TPU v7x, 256 devices: a whole 4x4x8 slice. The times are simulated.
256 devices in a mesh: row: 8 (over z_lo, y), col: 32 (over x, z_hi, core).
Axes of the slice: x: 4, y: 4, z: 8 (z_hi: 4, z_lo: 2; z = z_hi * 2 + z_lo), core: 2. Of those that a mesh axis runs over, the one named last changes fastest.
Arguments:
- density: bfloat16 [24576, 12288], P('row', 'col'), may hold values from -1.5 to 1.5
- neighbours: int32 [384, 192], replicated, may hold values from 0 to 383, as said below
- panels: int32 [2], replicated, may hold values from 0 to 31
Outputs:
- square_part: bfloat16 [24576, 12288], P('row', 'col')
Inputs may be any that keep to these rules, and one draw needn't show every extreme that they name: In each row of neighbours, the 6 entries of every group c are distinct and lie in [c * 12, (c + 1) * 12); block row i always holds its own diagonal block i.
All inputs are finite; a program needn't handle non-finite values.
Results may differ from a plain program's by a relative error of at most 0.001.
Values may be sent and summed in bfloat16 or wider, within the bound.
No kernel may reach another device: no remote copies, remote signals or barrier semaphores. Data moves between devices by JAX's collectives and lax.ppermute only.
A program may use at most 128 MiB of HBM per device.

v0:
```python
import jax
import jax.numpy as jnp
from jax import lax
from jax.sharding import PartitionSpec as P

BLK = 64
CB = 12


def spread(shard, axis, root):
    mine = lax.axis_index(axis) == root
    return lax.psum(jnp.where(mine, shard, jnp.zeros_like(shard)), axis)


def expand(values, columns, width_blocks):
    row_count = columns.shape[0]
    slot_count = columns.shape[1]
    shaped = values.reshape(row_count, BLK, slot_count, BLK)
    onehot = (
        columns[:, :, None] == jnp.arange(width_blocks, dtype=jnp.int32)[None, None, :]
    ).astype(jnp.bfloat16)
    dense_tile = jnp.einsum("iasb,isj->iajb", shaped, onehot, preferred_element_type=jnp.float32)
    return dense_tile.astype(jnp.bfloat16).reshape(row_count * BLK, width_blocks * BLK)


def on_device(density, neighbours, panels):
    row_blocks = density.shape[0] // BLK
    slot_count = density.shape[1] // BLK
    col_index = lax.axis_index("col")
    row_index = lax.axis_index("row")
    per_row = lax.axis_size("col") // lax.axis_size("row")
    my_rows = lax.dynamic_slice_in_dim(neighbours, row_index * row_blocks, row_blocks, 0)
    own_cols = (
        lax.dynamic_slice_in_dim(my_rows, col_index * slot_count, slot_count, 1) - col_index * CB
    )
    own_dense = expand(density, own_cols, CB)

    def fetch(number):
        owner_row = number // per_row
        offset = number % per_row * CB
        band_dense = lax.dynamic_slice_in_dim(own_dense, offset * BLK, CB * BLK, 0)
        left_dense = spread(own_dense, "col", number)
        right_dense = spread(band_dense, "row", owner_row)
        return (left_dense, right_dense)

    first_left, first_right = fetch(panels[0])
    second_left, second_right = fetch(panels[1])
    summed = jnp.dot(first_left, first_right, preferred_element_type=jnp.float32)
    summed = summed + jnp.dot(second_left, second_right, preferred_element_type=jnp.float32)
    rounded = summed.astype(jnp.bfloat16).reshape(row_blocks, BLK, CB, BLK)
    onehot = (own_cols[:, :, None] == jnp.arange(CB, dtype=jnp.int32)[None, None, :]).astype(
        jnp.bfloat16
    )
    picked = jnp.einsum("iajb,isj->iasb", rounded, onehot, preferred_element_type=jnp.float32)
    return picked.astype(jnp.bfloat16).reshape(row_blocks * BLK, slot_count * BLK)


def solution(mesh):
    return jax.shard_map(
        on_device,
        mesh=mesh,
        in_specs=(P("row", "col"), P(), P()),
        out_specs=P("row", "col"),
        check_vma=False,
    )
```

profile of v0, /device:TPU:32, one launch (start us, length us, event | category | flops | bytes accessed | tf_op | source)
XLA Modules:
  0.0 545.0 jit_solution(11395007383363114661)
XLA Ops:
  6.5 0.0 all-reduce.7.cloned.1.call-start
  6.5 1.3 fusion.5
  12.7 0.8 dynamic-slice_subtract_fusion
  13.5 0.1 copy.5
  13.6 8.2 %reshape.18 = bf16[48,64,6,64]{3,2,1,0:T(8,128)(2,1)} reshape(bf16[3072,384]{1,0:T(8,128)(2,1)} %param.3) | data formatting | bytes 4718592 | tf_op jit(solution)/shard_map/reshape | solution.py:18
  21.7 12.4 %convert_bitcast_fusion = bf16[48,64,12,64]{3,2,1,0:T(8,128)(2,1)} fusion(bf16[48,64,6,64]{3,2,1,0:T(8,128)(2,1)} %reshape.18, s32[48,6]{1,0:T(8,128)S(1)} %copy.5), kind=kOutput, calls=%fused_computation | convolution fusion | flops 30674304 | bytes 7079040 | tf_op jit(solution)/shard_map/iasb,isj->iajb/dot_general | solution.py:22
  34.1 15.6 %reshape.19 = bf16[3072,768]{1,0:T(8,128)(2,1)} reshape(bf16[48,64,12,64]{3,2,1,0:T(8,128)(2,1)} %convert_bitcast_fusion) | data formatting | bytes 9437184 | tf_op jit(solution)/shard_map/reshape | solution.py:23
  49.7 6.6 %copy.15 = bf16[3072,768]{0,1:T(8,128)(2,1)} copy(bf16[3072,768]{1,0:T(8,128)(2,1)} %reshape.19) | data formatting | bytes 9437184 | tf_op jit(solution)/shard_map/reshape | solution.py:23
  56.4 3.6 dynamic-slice_select_fusion
  59.9 0.0 all-reduce.7.cloned.1.call-update
  60.0 0.2 all-reduce.5.cloned.1.call-start
  61.4 6.5 %broadcast_select_fusion = (bf16[3072,768]{0,1:T(8,128)(2,1)}, bf16[3072,768]{0,1:T(8,128)(2,1)}) fusion(bf16[3072,768]{0,1:T(8,128)(2,1)} %copy.15, pred[]{:T(512)S(6)} %eq.40, pred[]{:T(512)S(6)} %eq.38), kind=kLoop, calls=%fused_computation.3 | loop fusion | flops 4718592 | bytes 14155778 | tf_op jit(solution)/shard_map/jit(_where)/select_n | solution.py:12
  67.9 0.0 all-reduce.5.cloned.1.call-update
  67.9 82.7 %all-reduce.7.cloned.1.call-done = (bf16[768,768]{0,1:T(8,128)(2,1)}, bf16[768,768]{0,1:T(8,128)(2,1)}) async-done(((bf16[768,768]{0,1:T(8,128)(2,1)}, bf16[768,768]{0,1:T(8,128)(2,1)}), (bf16[768,768]{0,1:T(8,128)(2,1)}, bf16[768,768]{0,1:T(8,128)(2,1)})) %all-reduce.7.cloned.1.call-update) | async-done | bytes 2359312 | tf_op jit(solution)/shard_map/psum | solution.py:12
  150.6 342.6 %all-reduce.5.cloned.1.call-done = (bf16[3072,768]{0,1:T(8,128)(2,1)}, bf16[3072,768]{0,1:T(8,128)(2,1)}) async-done(((bf16[3072,768]{0,1:T(8,128)(2,1)}, bf16[3072,768]{0,1:T(8,128)(2,1)}), (bf16[3072,768]{0,1:T(8,128)(2,1)}, bf16[3072,768]{0,1:T(8,128)(2,1)})) %all-reduce.5.cloned.1.call-update) | async-done | bytes 9437200 | tf_op jit(solution)/shard_map/psum | solution.py:12
  493.1 0.0 copy-start
  493.1 0.0 copy-start.1
  493.1 6.4 %fusion.6 = f32[3072,768]{1,0:T(8,128)S(1)} fusion(bf16[3072,768]{0,1:T(8,128)(2,1)} %get-tuple-element.5, bf16[768,768]{0,1:T(8,128)(2,1)} %get-tuple-element.7), kind=kOutput, calls=%fused_computation.13 | convolution fusion | flops 3623878656 | bytes 15335424 | tf_op jit(solution)/shard_map/dot_general | solution.py:48
  499.5 0.0 copy-done
  499.5 0.0 copy-done.1
  499.5 5.9 %add_convert_fusion = bf16[3072,768]{1,0:T(8,128)(2,1)} fusion(f32[3072,768]{1,0:T(8,128)S(1)} %fusion.6, bf16[3072,768]{0,1:T(8,128)(2,1)S(1)} %copy-done, bf16[768,768]{0,1:T(8,128)(2,1)S(1)} %copy-done.1), kind=kOutput, calls=%fused_computation.1 | convolution fusion | flops 3628597248 | bytes 20054016 | tf_op jit(solution)/shard_map/dot_general | solution.py:49
  505.4 15.0 %reshape.20 = bf16[48,64,12,64]{3,2,1,0:T(8,128)(2,1)} reshape(bf16[3072,768]{1,0:T(8,128)(2,1)} %add_convert_fusion) | data formatting | bytes 9437184 | tf_op jit(solution)/shard_map/reshape | solution.py:50
  520.4 9.0 %convert_bitcast_fusion.1 = bf16[48,64,6,64]{3,2,1,0:T(8,128)(2,1)} fusion(bf16[48,64,12,64]{3,2,1,0:T(8,128)(2,1)} %reshape.20, s32[48,6]{1,0:T(8,128)S(1)} %copy.5), kind=kOutput, calls=%fused_computation.2 | convolution fusion | flops 29494656 | bytes 7079040 | tf_op jit(solution)/shard_map/iajb,isj->iasb/dot_general | solution.py:54
  529.4 8.7 %reshape.21 = bf16[3072,384]{1,0:T(8,128)(2,1)} reshape(bf16[48,64,6,64]{3,2,1,0:T(8,128)(2,1)} %convert_bitcast_fusion.1) | data formatting | bytes 4718592 | tf_op jit(solution)/shard_map/reshape | solution.py:55
Async XLA Ops:
  6.5 144.0 %all-reduce.7.cloned.1.call-start = ((), (), s32[]{:S(2)}) async-start(), calls=%async_computation.1 | async-start | bytes 4718592 | tf_op jit(solution)/shard_map/psum | solution.py:12
  60.0 433.2 %all-reduce.5.cloned.1.call-start = ((), (), s32[]{:S(2)}) async-start(), calls=%async_computation | async-start | bytes 18874368 | tf_op jit(solution)/shard_map/psum | solution.py:12
  493.1 6.4 %copy-start = (bf16[3072,768]{0,1:T(8,128)(2,1)S(1)}, bf16[3072,768]{0,1:T(8,128)(2,1)}, u32[]{:S(2)}) copy-start(bf16[3072,768]{0,1:T(8,128)(2,1)} %get-tuple-element.6) | copy-start | bytes 14155780
  493.1 6.4 %copy-start.1 = (bf16[768,768]{0,1:T(8,128)(2,1)S(1)}, bf16[768,768]{0,1:T(8,128)(2,1)}, u32[]{:S(2)}) copy-start(bf16[768,768]{0,1:T(8,128)(2,1)} %get-tuple-element.8) | copy-start | bytes 3538948
Sparse Core Ops, SparseCore 0:
  60.1 90.4 all-reduce.6
  153.3 339.7 all-reduce.4
where the time goes:
time: 547 us; the launch traced here: 545 us
  waiting for transfers between devices  425 us (78%)
  local copies, waits for them, and re-layouts  55.5 us (10%)
  matrix products  33.7 us (6%)
  between operations  19.4 us (4%)
  other arithmetic  10.9 us (2%)
    psum x2, waiting for transfers between devices, spread(): return lax.psum(jnp.where(mine, shard, jnp.zeros_like(shard)), axis)  425 us
    reshape x2, local copies, waits for them, and re-layouts, expand(): dense_tile.astype(jnp.bfloat16).reshape(row_count * BLK, width_blocks * BLK)  22.2 us
    reshape x1, local copies, waits for them, and re-layouts, on_device(): rounded = summed.astype(jnp.bfloat16).reshape(row_blocks, BLK, CB, BLK)  15 us
    dot_general x1, matrix products, expand(): jnp.einsum('iasb,isj->iajb', shaped, onehot, preferred_element_type=jnp.f...  12.4 us
  transfers between devices with their start and end apart: 2, of which 2 were waited for; matrix products, arithmetic and copies ran while one was open for 1% of the time, Pallas kernels for 0%

commit v1 on v0

v1 whole, which is shorter than its diff:
```python
import jax
import jax.numpy as jnp
from jax import lax
from jax.sharding import Mesh
from jax.sharding import PartitionSpec as P

BLK = 64
CB = 12
ROW_AXES = ("rz", "ry")
COL_AXES = ("cx", "cz", "cc")


def expand(values, columns, width_blocks):
    row_count, slot_count = columns.shape
    shaped = values.reshape(row_count, BLK, 1, slot_count, BLK)
    hit = columns[:, None, None, :, None] == jnp.arange(width_blocks, dtype=jnp.int32)[None, None, :, None, None]
    dense = jnp.where(hit, shaped, jnp.zeros((), values.dtype)).sum(axis=3, dtype=values.dtype)
    return dense.reshape(row_count * BLK, width_blocks * BLK)


def pick(dense, columns):
    row_count, slot_count = columns.shape
    width_blocks = dense.shape[1] // BLK
    shaped = dense.reshape(row_count, BLK, 1, width_blocks, BLK)
    hit = columns[:, None, :, None, None] == jnp.arange(width_blocks, dtype=jnp.int32)[None, None, None, :, None]
    picked = jnp.where(hit, shaped, jnp.zeros((), dense.dtype)).sum(axis=3, dtype=dense.dtype)
    return picked.reshape(row_count * BLK, slot_count * BLK)


def ring_shift(x, axis, size, step):
    return lax.ppermute(x, axis, [(i, (i + step) % size) for i in range(size)])


def row_broadcast(buf, root_z, root_y):
    z = lax.axis_index("rz")
    y = lax.axis_index("ry")
    ny = lax.axis_size("ry")
    got = ring_shift(buf, "rz", 2, 1)
    buf = jnp.where((z == root_z)[:, None, None], buf, got)
    dist = ((y - root_y + ny) % ny)[:, None, None]
    from_left = ring_shift(buf, "ry", ny, 1)
    from_right = ring_shift(buf, "ry", ny, -1)
    buf = jnp.where(dist == 1, from_left, jnp.where(dist == ny - 1, from_right, buf))
    half = buf.shape[1] // 2
    first = ring_shift(buf[:, :half], "ry", ny, 1)
    second = ring_shift(buf[:, half:], "ry", ny, -1)
    far = jnp.concatenate([first, second], axis=1)
    return jnp.where(dist == 2, far, buf)


def on_device(density, neighbours, panels):
    row_blocks = density.shape[0] // BLK
    slot_count = density.shape[1] // BLK
    col_index = (lax.axis_index("cx") * lax.axis_size("cz") + lax.axis_index("cz")) * lax.axis_size(
        "cc"
    ) + lax.axis_index("cc")
    row_index = lax.axis_index("rz") * lax.axis_size("ry") + lax.axis_index("ry")
    n_col = lax.axis_size("cx") * lax.axis_size("cz") * lax.axis_size("cc")
    panels_per_row = n_col // (lax.axis_size("rz") * lax.axis_size("ry"))
    my_rows = lax.dynamic_slice_in_dim(neighbours, row_index * row_blocks, row_blocks, 0)
    own_cols = lax.dynamic_slice_in_dim(my_rows, col_index * slot_count, slot_count, 1) - col_index * CB

    lefts = []
    bands = []
    for s in range(2):
        number = panels[s]
        lefts.append(jnp.where(col_index == number, density, jnp.zeros_like(density)))
        offset = number % panels_per_row * CB * BLK
        band = lax.dynamic_slice_in_dim(density, offset, CB * BLK, 0)
        bands.append(jnp.where(row_index == number // panels_per_row, band, jnp.zeros_like(band)))

    stacked = jnp.stack(lefts).reshape(2 * density.shape[0], density.shape[1])
    part = lax.psum_scatter(stacked, COL_AXES, scatter_dimension=0, tiled=True)
    left_all = lax.all_gather(part, COL_AXES, axis=0, tiled=True).reshape(2, *density.shape)

    band_all = jnp.stack(bands)
    owner_row = panels // panels_per_row
    n_ry = lax.axis_size("ry")
    band_all = row_broadcast(band_all, owner_row // n_ry, owner_row % n_ry)

    left_dense = []
    right_dense = []
    for s in range(2):
        number = panels[s]
        group_cols = lax.dynamic_slice_in_dim(my_rows, number * slot_count, slot_count, 1) - number * CB
        left_dense.append(expand(left_all[s], group_cols, CB))
        band_rows = lax.dynamic_slice_in_dim(neighbours, number * CB, CB, 0)
        band_cols = lax.dynamic_slice_in_dim(band_rows, col_index * slot_count, slot_count, 1) - col_index * CB
        right_dense.append(expand(band_all[s], band_cols, CB))
    summed = jnp.dot(
        jnp.concatenate(left_dense, axis=1),
        jnp.concatenate(right_dense, axis=0),
        preferred_element_type=jnp.float32,
    )
    rounded = summed.astype(jnp.bfloat16)
    return pick(rounded, own_cols)


def solution(mesh):
    n_row, n_col = mesh.devices.shape
    sub = Mesh(mesh.devices.reshape(2, n_row // 2, 4, n_col // 8, 2), ROW_AXES + COL_AXES)
    return jax.shard_map(
        on_device,
        mesh=sub,
        in_specs=(P(ROW_AXES, COL_AXES), P(), P()),
        out_specs=P(ROW_AXES, COL_AXES),
        check_vma=False,
    )
```

time: 547 us -> 463 us (0.85); the launches traced: 545 us -> 455 us
  waiting for transfers between devices: 425 us -> 158 us
  local copies, waits for them, and re-layouts: 55.5 us -> 150 us
  other arithmetic: 10.9 us -> 105 us
  matrix products: 33.7 us -> 11.6 us
  starting transfers between devices: 0.22 us -> 7.93 us
    psum x2 -> x0, waiting for transfers between devices: 425 us -> none  [spread(): return lax.psum(jnp.where(mine, shard, jnp.zeros_like(shard)), axis)]
    reduce_scatter x0 -> x1, waiting for transfers between devices: none -> 104 us  [on_device(): part = lax.psum_scatter(stacked, COL_AXES, scatter_dimension=0, tiled=True)]
    reduce_sum x0 -> x5, other arithmetic: none -> 90.5 us  [the longest x4 59.9 us: expand(): jnp.where(hit, shaped, jnp.zeros((), values.dtype))]
    broadcast_in_dim x0 -> x10, local copies, waits for them, and re-layouts: none -> 56.3 us  [the longest x8 30.6 us: expand(): jnp.where(hit, shaped, jnp.zeros((), values.dtype))]
    ppermute x0 -> x5, waiting for transfers between devices: none -> 54.2 us  [ring_shift(): return lax.ppermute(x, axis, [(i, (i + step) % size) for i in range(size)])]
    reduce_sum x0 -> x4, local copies, waits for them, and re-layouts: none -> 30.5 us  [expand(): jnp.where(hit, shaped, jnp.zeros((), values.dtype))]
    dot_general x4 -> x1, matrix products: 33.7 us -> 11.6 us  [on_device(): jnp.dot(jnp.concatenate(left_dense, axis=1), jnp.concatenate(right_dense,...]
    ppermute x0 -> x5, starting transfers between devices: none -> 7.89 us  [ring_shift(): return lax.ppermute(x, axis, [(i, (i + step) % size) for i in range(size)])]
  transfers between devices with their start and end apart: 2 -> 7, of which waited for: 2 -> 6; matrix products, arithmetic and copies ran while one was open for 1% -> 8% of each run, Pallas kernels for 0% -> 0%
where the time goes in v1:
time: 463 us; the launch traced here: 455 us
  waiting for transfers between devices  158 us (34%)
  local copies, waits for them, and re-layouts  150 us (32%)
  other arithmetic  105 us (23%)
  between operations  22.3 us (5%)
  matrix products  11.6 us (3%)
  starting transfers between devices  7.93 us (2%)
    reduce_scatter x1, waiting for transfers between devices, on_device(): part = lax.psum_scatter(stacked, COL_AXES, scatter_dimension=0, tiled=True)  104 us
    reduce_sum x4, other arithmetic, expand(): jnp.where(hit, shaped, jnp.zeros((), values.dtype))  59.9 us
    ppermute x5, waiting for transfers between devices, ring_shift(): return lax.ppermute(x, axis, [(i, (i + step) % size) for i in range(size)])  54.2 us
    reshape x4, local copies, waits for them, and re-layouts, expand(): return dense.reshape(row_count * BLK, width_blocks * BLK)  30.8 us
    reduce_sum x1, other arithmetic, pick(): jnp.where(hit, shaped, jnp.zeros((), dense.dtype))  30.6 us
    broadcast_in_dim x8, local copies, waits for them, and re-layouts, expand(): jnp.where(hit, shaped, jnp.zeros((), values.dtype))  30.6 us
    reduce_sum x4, local copies, waits for them, and re-layouts, expand(): jnp.where(hit, shaped, jnp.zeros((), values.dtype))  30.5 us
    broadcast_in_dim x2, local copies, waits for them, and re-layouts, pick(): jnp.where(hit, shaped, jnp.zeros((), dense.dtype))  25.7 us
  transfers between devices with their start and end apart: 7, of which 6 were waited for; matrix products, arithmetic and copies ran while one was open for 8% of the time, Pallas kernels for 0%

profile of v1, /device:TPU:32, one launch (start us, length us, event | category | flops | bytes accessed | tf_op | source)
XLA Modules:
  0.0 455.0 jit_solution(5181201618885722683)
XLA Ops:
  9.1 2.1 select_bitcast_fusion.1
  11.1 2.7 pad_maximum_fusion
  13.9 104.1 %reduce-scatter.4.cloned.1.call-done = bf16[192,384]{1,0:T(8,128)(2,1)} async-done(((bf16[6144,384]{1,0:T(8,128)(2,1)}), bf16[192,384]{1,0:T(8,128)(2,1)}) %reduce-scatter.4.cloned.1.call-update) | async-done | bytes 147472 | tf_op jit(solution)/shard_map/reduce_scatter | solution.py:73
  123.2 1.8 collective-permute-start
  125.7 28.5 %collective-permute-done = bf16[2,768,384]{2,1,0:T(8,128)(2,1)S(1)} collective-permute-done((bf16[2,768,384]{2,1,0:T(8,128)(2,1)S(1)}, bf16[2,768,384]{2,1,0:T(8,128)(2,1)S(1)}, u32[]{:S(2)}, u32[]{:S(2)}) %collective-permute-start) | collective-permute-done | bytes 1179680 | tf_op jit(solution)/shard_map/ppermute | solution.py:31
  169.2 13.0 %collective-permute-done.1 = bf16[2,768,384]{2,1,0:T(8,128)(2,1)S(1)} collective-permute-done((bf16[2,768,384]{2,1,0:T(8,128)(2,1)}, bf16[2,768,384]{2,1,0:T(8,128)(2,1)S(1)}, u32[]{:S(2)}, u32[]{:S(2)}) %collective-permute-start.1) | collective-permute-done | bytes 1179680 | tf_op jit(solution)/shard_map/ppermute | solution.py:31
  184.3 2.8 collective-permute-start.4
  187.3 8.9 %collective-permute-done.4 = bf16[2,384,384]{2,1,0:T(8,128)(2,1)S(1)} collective-permute-done((bf16[2,384,384]{2,1,0:T(8,128)(2,1)S(1)}, bf16[2,384,384]{2,1,0:T(8,128)(2,1)S(1)}, u32[]{:S(2)}, u32[]{:S(2)}) %collective-permute-start.4) | collective-permute-done | bytes 589856 | tf_op jit(solution)/shard_map/ppermute | solution.py:31
  196.2 3.4 collective-permute-done.3
  202.4 5.3 %select_reduce_fusion.3 = bf16[12,64,12,64]{3,1,2,0:T(8,128)(2,1)S(1)} fusion(pred[12,12,6]{2,1,0:T(8,128)(4,1)S(1)} %copy-done.4, bf16[12,64,6,64]{3,1,2,0:T(8,128)(2,1)S(1)} %copy.49), kind=kLoop, calls=%fused_computation.3 | loop fusion | flops 6488064 | bytes 1770336 | tf_op jit(solution)/shard_map/reduce_sum | solution.py:17
  209.6 2.8 reshape.80
  212.3 2.2 broadcast_in_dim.140
  214.9 5.3 %select_reduce_fusion.4 = bf16[12,64,12,64]{3,1,2,0:T(8,128)(2,1)S(1)} fusion(pred[12,12,6]{2,1,0:T(8,128)(4,1)S(1)} %iota_compare_fusion.4, bf16[12,64,6,64]{3,1,2,0:T(8,128)(2,1)S(1)} %copy.46), kind=kLoop, calls=%fused_computation.4 | loop fusion | flops 6488064 | bytes 1770336 | tf_op jit(solution)/shard_map/reduce_sum | solution.py:17
  220.2 1.8 copy.47
  222.1 2.8 reshape.79
  224.9 4.3 fusion.15
  229.2 8.1 %reshape.83 = bf16[48,64,6,64]{3,2,1,0:T(8,128)(2,1)} reshape(bf16[3072,384]{1,0:T(8,128)(2,1)} %get-tuple-element.9) | data formatting | bytes 4718592 | tf_op jit(solution)/shard_map/jit(_where)/broadcast_in_dim | solution.py:17
  237.3 6.4 %copy.43 = bf16[48,64,6,64]{3,1,2,0:T(8,128)(2,1)} copy(bf16[48,64,6,64]{3,2,1,0:T(8,128)(2,1)} %reshape.83) | data formatting | bytes 4718592 | tf_op jit(solution)/shard_map/jit(_where)/broadcast_in_dim | solution.py:17
  243.7 24.8 %select_reduce_fusion.1 = bf16[48,64,12,64]{3,1,2,0:T(8,128)(2,1)} fusion(pred[48,12,6]{2,1,0:T(8,128)(4,1)S(1)} %iota_compare_fusion, bf16[48,64,6,64]{3,1,2,0:T(8,128)(2,1)} %copy.43), kind=kLoop, calls=%fused_computation.1 | loop fusion | flops 25952256 | bytes 7081344 | tf_op jit(solution)/shard_map/reduce_sum | solution.py:17
  268.5 13.4 %copy.44 = bf16[48,64,12,64]{1,0,3,2:T(8,128)(2,1)} copy(bf16[48,64,12,64]{3,1,2,0:T(8,128)(2,1)} %select_reduce_fusion.1) | data formatting | bytes 9437184 | tf_op jit(solution)/shard_map/reduce_sum | solution.py:17
  282.0 12.5 %reshape.78 = bf16[3072,768]{0,1:T(8,128)(2,1)} reshape(bf16[48,64,12,64]{1,0,3,2:T(8,128)(2,1)} %copy.44) | data formatting | bytes 9437184 | tf_op jit(solution)/shard_map/reshape | solution.py:18
  294.5 5.7 %reshape.82 = bf16[48,64,6,64]{3,2,1,0:T(8,128)(2,1)} reshape(bf16[3072,384]{1,0:T(8,128)(2,1)S(1)} %get-tuple-element.8) | data formatting | bytes 4718592 | tf_op jit(solution)/shard_map/jit(_where)/broadcast_in_dim | solution.py:17
  300.2 6.4 %copy.39 = bf16[48,64,6,64]{3,1,2,0:T(8,128)(2,1)} copy(bf16[48,64,6,64]{3,2,1,0:T(8,128)(2,1)} %reshape.82) | data formatting | bytes 4718592 | tf_op jit(solution)/shard_map/jit(_where)/broadcast_in_dim | solution.py:17
  306.6 24.4 %select_reduce_fusion.2 = bf16[48,64,12,64]{3,1,2,0:T(8,128)(2,1)} fusion(pred[48,12,6]{2,1,0:T(8,128)(4,1)S(1)} %iota_compare_fusion.1, bf16[48,64,6,64]{3,1,2,0:T(8,128)(2,1)} %copy.39), kind=kLoop, calls=%fused_computation.2 | loop fusion | flops 25952256 | bytes 7081344 | tf_op jit(solution)/shard_map/reduce_sum | solution.py:17
  331.0 13.4 %copy.40 = bf16[48,64,12,64]{1,0,3,2:T(8,128)(2,1)} copy(bf16[48,64,12,64]{3,1,2,0:T(8,128)(2,1)} %select_reduce_fusion.2) | data formatting | bytes 9437184 | tf_op jit(solution)/shard_map/reduce_sum | solution.py:17
  344.5 12.7 %reshape.77 = bf16[3072,768]{0,1:T(8,128)(2,1)} reshape(bf16[48,64,12,64]{1,0,3,2:T(8,128)(2,1)} %copy.40) | data formatting | bytes 9437184 | tf_op jit(solution)/shard_map/reshape | solution.py:18
  357.1 11.6 %fusion.4 = bf16[3072,768]{1,0:T(8,128)(2,1)} fusion(bf16[3072,768]{0,1:T(8,128)(2,1)} %reshape.78, bf16[3072,768]{0,1:T(8,128)(2,1)} %reshape.77, bf16[768,768]{1,0:T(8,128)(2,1)S(1)} %copy-done.1, bf16[768,768]{1,0:T(8,128)(2,1)S(1)} %copy-done.2), kind=kOutput, calls=%fused_computation.9 | convolution fusion | flops 7273709568 | bytes 16515072 | tf_op jit(solution)/shard_map/dot_general | solution.py:90
  368.7 15.1 %reshape.84 = bf16[48,64,12,64]{3,2,1,0:T(8,128)(2,1)} reshape(bf16[3072,768]{1,0:T(8,128)(2,1)} %fusion.4) | data formatting | bytes 9437184 | tf_op jit(solution)/shard_map/jit(_where)/broadcast_in_dim | solution.py:26
  383.8 10.6 %copy.52 = bf16[48,64,12,64]{3,1,2,0:T(8,128)(2,1)} copy(bf16[48,64,12,64]{3,2,1,0:T(8,128)(2,1)} %reshape.84) | data formatting | bytes 9437184 | tf_op jit(solution)/shard_map/jit(_where)/broadcast_in_dim | solution.py:26
  394.4 30.6 %select_reduce_fusion = bf16[48,64,6,64]{3,1,2,0:T(8,128)(2,1)} fusion(pred[48,6,12]{2,1,0:T(8,128)(4,1)S(1)} %copy-done.3, bf16[48,64,12,64]{3,1,2,0:T(8,128)(2,1)} %copy.52), kind=kLoop, calls=%fused_computation | loop fusion | flops 27131904 | bytes 7081344 | tf_op jit(solution)/shard_map/reduce_sum | solution.py:26
  425.0 14.3 %copy.62 = bf16[48,64,6,64]{3,2,1,0:T(8,128)(2,1)} copy(bf16[48,64,6,64]{3,1,2,0:T(8,128)(2,1)} %select_reduce_fusion) | data formatting | bytes 4718592 | tf_op jit(solution)/shard_map/reshape | solution.py:27
  439.2 8.7 %reshape.85 = bf16[3072,384]{1,0:T(8,128)(2,1)} reshape(bf16[48,64,6,64]{3,2,1,0:T(8,128)(2,1)} %copy.62) | data formatting | bytes 4718592 | tf_op jit(solution)/shard_map/reshape | solution.py:27
  (56 shorter events, 22.0 us)
Async XLA Ops:
  6.5 111.5 %reduce-scatter.4.cloned.1.call-start = ((), (), s32[]{:S(2)}) async-start(), calls=%async_computation.2 | async-start | bytes 4866048 | tf_op jit(solution)/shard_map/reduce_scatter | solution.py:73
  13.8 109.1 %copy-start = (bf16[3072,384]{1,0:T(8,128)(2,1)S(1)}, bf16[3072,384]{1,0:T(8,128)(2,1)}, u32[]{:S(2)}) copy-start(bf16[3072,384]{1,0:T(8,128)(2,1)} %param.3) | copy-start | bytes 7077892
  13.8 211.1 %all-gather.2.cloned.1.call-start = ((), (), s32[]{:S(2)}) async-start(), calls=%async_computation.1 | async-start | bytes 4866048 | tf_op jit(solution)/shard_map/all_gather | solution.py:74
  122.9 2.2 copy-start.7
  123.2 31.0 %collective-permute-start = (bf16[2,768,384]{2,1,0:T(8,128)(2,1)S(1)}, bf16[2,768,384]{2,1,0:T(8,128)(2,1)S(1)}, u32[]{:S(2)}, u32[]{:S(2)}) collective-permute-start(bf16[2,768,384]{2,1,0:T(8,128)(2,1)S(1)} %pad_maximum_fusion.1), channel_id=1, source_target_pairs={{0,128},{128,0},{1,129},{129,1},{2,130},{130,2},{3,131},{131,3},{4... | collective-permute-start | bytes 3538952 | tf_op jit(solution)/shard_map/ppermute | solution.py:31
  125.7 28.5 %copy-start.8 = (pred[2]{0:T(512)(128)(4,1)}, pred[2]{0:T(512)(128)(4,1)S(1)}, u32[]{:S(2)}) copy-start(pred[2]{0:T(512)(128)(4,1)S(1)} %fusion.13) | copy-start | bytes 10
  155.5 26.7 %collective-permute-start.1 = (bf16[2,768,384]{2,1,0:T(8,128)(2,1)}, bf16[2,768,384]{2,1,0:T(8,128)(2,1)S(1)}, u32[]{:S(2)}, u32[]{:S(2)}) collective-permute-start(bf16[2,768,384]{2,1,0:T(8,128)(2,1)} %broadcast_select_fusion), channel_id=1, source_target_pairs={{0,32},{32,64},{64,96},{96,0},{1,33},{33,65},{65,97},{97,1},{2,34}... | collective-permute-start | bytes 3538952 | tf_op jit(solution)/shard_map/ppermute | solution.py:31
  157.1 25.5 %collective-permute-start.2 = (bf16[2,768,384]{2,1,0:T(8,128)(2,1)}, bf16[2,768,384]{2,1,0:T(8,128)(2,1)}, u32[]{:S(2)}, u32[]{:S(2)}) collective-permute-start(bf16[2,768,384]{2,1,0:T(8,128)(2,1)} %broadcast_select_fusion), channel_id=1, source_target_pairs={{0,96},{32,0},{64,32},{96,64},{1,97},{33,1},{65,33},{97,65},{2,98}... | collective-permute-start | bytes 3538952 | tf_op jit(solution)/shard_map/ppermute | solution.py:31
  184.1 3.0 copy-start.5
  184.1 3.1 copy-start.6
  184.1 15.4 %copy-start.9 = (pred[2]{0:T(512)(128)(4,1)S(1)}, pred[2]{0:T(512)(128)(4,1)}, u32[]{:S(2)}) copy-start(pred[2]{0:T(512)(128)(4,1)} %get-tuple-element.5) | copy-start | bytes 10
  184.3 11.9 %collective-permute-start.4 = (bf16[2,384,384]{2,1,0:T(8,128)(2,1)S(1)}, bf16[2,384,384]{2,1,0:T(8,128)(2,1)S(1)}, u32[]{:S(2)}, u32[]{:S(2)}) collective-permute-start(bf16[2,384,384]{2,1,0:T(8,128)(2,1)S(1)} %get-tuple-element.17), channel_id=1, source_target_pairs={{0,96},{32,0},{64,32},{96,64},{1,97},{33,1},{65,33},{97,65},{2,98}... | collective-permute-start | bytes 1769480 | tf_op jit(solution)/shard_map/ppermute | solution.py:31
  187.1 12.5 %collective-permute-start.3 = (bf16[2,384,384]{2,1,0:T(8,128)(2,1)S(1)}, bf16[2,384,384]{2,1,0:T(8,128)(2,1)S(1)}, u32[]{:S(2)}, u32[]{:S(2)}) collective-permute-start(bf16[2,384,384]{2,1,0:T(8,128)(2,1)S(1)} %get-tuple-element.16), channel_id=1, source_target_pairs={{0,32},{32,64},{64,96},{96,0},{1,33},{33,65},{65,97},{97,1},{2,34}... | collective-permute-start | bytes 1769480 | tf_op jit(solution)/shard_map/ppermute | solution.py:31
  201.0 1.4 copy-start.4
  344.5 12.7 %copy-start.1 = (bf16[768,768]{1,0:T(8,128)(2,1)S(1)}, bf16[768,768]{1,0:T(8,128)(2,1)}, u32[]{:S(2)}) copy-start(bf16[768,768]{1,0:T(8,128)(2,1)} %reshape.80) | copy-start | bytes 3538948
  344.5 12.7 %copy-start.2 = (bf16[768,768]{1,0:T(8,128)(2,1)S(1)}, bf16[768,768]{1,0:T(8,128)(2,1)}, u32[]{:S(2)}) copy-start(bf16[768,768]{1,0:T(8,128)(2,1)} %reshape.79) | copy-start | bytes 3538948
  383.8 10.6 %copy-start.3 = (pred[48,6,12]{2,1,0:T(8,128)(4,1)S(1)}, pred[48,6,12]{2,1,0:T(8,128)(4,1)}, u32[]{:S(2)}) copy-start(pred[48,6,12]{2,1,0:T(8,128)(4,1)} %iota_compare_fusion.2) | copy-start | bytes 10372
Sparse Core Ops, SparseCore 0:
  13.9 104.0 reduce-scatter.3
  120.5 61.4 all-gather.1

commit v2 on v1

--- a/solution.py
+++ b/solution.py
@@ -1,6 +1,10 @@
+import functools
+
 import jax
 import jax.numpy as jnp
 from jax import lax
+from jax.experimental import pallas as pl
+from jax.experimental.pallas import tpu as pltpu
 from jax.sharding import Mesh
 from jax.sharding import PartitionSpec as P
 
@@ -10,21 +14,67 @@
 COL_AXES = ("cx", "cz", "cc")
 
 
-def expand(values, columns, width_blocks):
-    row_count, slot_count = columns.shape
-    shaped = values.reshape(row_count, BLK, 1, slot_count, BLK)
-    hit = columns[:, None, None, :, None] == jnp.arange(width_blocks, dtype=jnp.int32)[None, None, :, None, None]
-    dense = jnp.where(hit, shaped, jnp.zeros((), values.dtype)).sum(axis=3, dtype=values.dtype)
-    return dense.reshape(row_count * BLK, width_blocks * BLK)
+def _halves(chunk):
+    wide = chunk.astype(jnp.float32)
+    return wide, pltpu.roll(wide, BLK, 1)
 
 
-def pick(dense, columns):
-    row_count, slot_count = columns.shape
-    width_blocks = dense.shape[1] // BLK
-    shaped = dense.reshape(row_count, BLK, 1, width_blocks, BLK)
-    hit = columns[:, None, :, None, None] == jnp.arange(width_blocks, dtype=jnp.int32)[None, None, None, :, None]
-    picked = jnp.where(hit, shaped, jnp.zeros((), dense.dtype)).sum(axis=3, dtype=dense.dtype)
-    return picked.reshape(row_count * BLK, slot_count * BLK)
+def _place_kernel(src_blocks, dst_blocks, tile_rows, block_rows, table, values, out):
+    step = pl.program_id(0)
+    tile = pl.program_id(1)
+    lanes = lax.broadcasted_iota(jnp.int32, (BLK, 2 * BLK), 1)
+    high = lanes >= BLK
+    half = lanes // BLK
+    placing = src_blocks < dst_blocks
+    entries = src_blocks if placing else dst_blocks
+    per_step = block_rows * entries
+    for q in range(tile_rows // BLK):
+        base = step * per_step + (tile * (tile_rows // BLK) + q) * entries
+        rows = pl.ds(q * BLK, BLK)
+        plain = []
+        swapped = []
+        for c in range(src_blocks // 2):
+            a, b = _halves(values[0, rows, pl.ds(c * 2 * BLK, 2 * BLK)])
+            plain.append(a)
+            swapped.append(b)
+        sources = []
+        for t in range(src_blocks):
+            own = plain[t // 2]
+            other = swapped[t // 2]
+            if t % 2 == 0:
+                sources.append(jnp.where(high, other, own))
+            else:
+                sources.append(jnp.where(high, own, other))
+        for p in range(dst_blocks // 2):
+            acc = jnp.zeros((BLK, 2 * BLK), jnp.float32)
+            for t in range(src_blocks):
+                if placing:
+                    hit = half + 2 * p == table[base + t]
+                else:
+                    hit = jnp.where(high, table[base + 2 * p + 1], table[base + 2 * p]) == t
+                acc = jnp.where(hit, sources[t], acc)
+            out[rows, pl.ds(p * 2 * BLK, 2 * BLK)] = acc.astype(out.dtype)
+
+
+def place(values, table, src_blocks, dst_blocks, tile_rows, by_rows):
+    steps, rows, _ = values.shape
+    tiles = rows // tile_rows
+    if not by_rows:
+        out_shape = (rows, steps * dst_blocks * BLK)
+        out_map = lambda s, g, tab: (g, s)
+    else:
+        out_shape = (steps * rows, dst_blocks * BLK)
+        out_map = lambda s, g, tab: (s * tiles + g, 0)
+    return pl.pallas_call(
+        functools.partial(_place_kernel, src_blocks, dst_blocks, tile_rows, rows // BLK),
+        out_shape=jax.ShapeDtypeStruct(out_shape, values.dtype),
+        grid_spec=pltpu.PrefetchScalarGridSpec(
+            num_scalar_prefetch=1,
+            grid=(steps, tiles),
+            in_specs=[pl.BlockSpec((1, tile_rows, src_blocks * BLK), lambda s, g, tab: (s, g, 0))],
+            out_specs=pl.BlockSpec((tile_rows, dst_blocks * BLK), out_map),
+        ),
+    )(table, values)
 
 
 def ring_shift(x, axis, size, step):
@@ -78,22 +128,19 @@
     n_ry = lax.axis_size("ry")
     band_all = row_broadcast(band_all, owner_row // n_ry, owner_row % n_ry)
 
-    left_dense = []
-    right_dense = []
+    left_tables = []
+    right_tables = []
     for s in range(2):
         number = panels[s]
         group_cols = lax.dynamic_slice_in_dim(my_rows, number * slot_count, slot_count, 1) - number * CB
-        left_dense.append(expand(left_all[s], group_cols, CB))
+        left_tables.append(group_cols.reshape(-1))
         band_rows = lax.dynamic_slice_in_dim(neighbours, number * CB, CB, 0)
         band_cols = lax.dynamic_slice_in_dim(band_rows, col_index * slot_count, slot_count, 1) - col_index * CB
-        right_dense.append(expand(band_all[s], band_cols, CB))
-    summed = jnp.dot(
-        jnp.concatenate(left_dense, axis=1),
-        jnp.concatenate(right_dense, axis=0),
-        preferred_element_type=jnp.float32,
-    )
-    rounded = summed.astype(jnp.bfloat16)
-    return pick(rounded, own_cols)
+        right_tables.append(band_cols.reshape(-1))
+    left_dense = place(left_all, jnp.concatenate(left_tables), slot_count, CB, 256, False)
+    right_dense = place(band_all, jnp.concatenate(right_tables), slot_count, CB, 256, True)
+    product = jnp.dot(left_dense, right_dense, preferred_element_type=jnp.float32).astype(jnp.bfloat16)
+    return place(product[None], own_cols.reshape(-1), CB, slot_count, 256, True)
 
 
 def solution(mesh):

time: 463 us -> 260 us (0.56); the launches traced: 455 us -> 257 us
  local copies, waits for them, and re-layouts: 150 us -> 8.28 us
  other arithmetic: 105 us -> 12.1 us
  Pallas kernels: 0 us -> 36.7 us
    reduce_sum x5 -> x0, other arithmetic: 90.5 us -> none  [the longest x4 59.9 us: expand(): jnp.where(hit, shaped, jnp.zeros((), values.dtype))]
    broadcast_in_dim x10 -> x0, local copies, waits for them, and re-layouts: 56.3 us -> none  [the longest x8 30.6 us: expand(): jnp.where(hit, shaped, jnp.zeros((), values.dtype))]
    reshape x6 -> x5, local copies, waits for them, and re-layouts: 53.8 us -> 4.48 us  [the longest x2 2.86 us: on_device(): left_tables.append(group_cols.reshape(-1))]
    pallas_call x0 -> x3, Pallas kernels: none -> 36.7 us  [place(): pl.pallas_call(functools.partial(_place_kernel, src_blocks, dst_blocks, t...]
    reduce_sum x4 -> x0, local copies, waits for them, and re-layouts: 30.5 us -> none  [expand(): jnp.where(hit, shaped, jnp.zeros((), values.dtype))]
    slice x2 -> x0, local copies, waits for them, and re-layouts: 5.19 us -> none  [the longest x1 4.25 us: on_device(): left_dense.append(expand(left_all[s], group_cols, CB))]
  transfers between devices with their start and end apart: 7 -> 7, of which waited for: 6 -> 4; matrix products, arithmetic and copies ran while one was open for 8% -> 6% of each run, Pallas kernels for 0% -> 2%
where the time goes in v2:
time: 260 us; the launch traced here: 257 us
  waiting for transfers between devices  157 us (60%)
  Pallas kernels  36.7 us (14%)
  between operations  22.6 us (9%)
  matrix products  12.8 us (5%)
  other arithmetic  12.1 us (5%)
  local copies, waits for them, and re-layouts  8.28 us (3%)
  starting transfers between devices  7.71 us (3%)
    reduce_scatter x1, waiting for transfers between devices, on_device(): part = lax.psum_scatter(stacked, COL_AXES, scatter_dimension=0, tiled=True)  104 us
    ppermute x5, waiting for transfers between devices, ring_shift(): return lax.ppermute(x, axis, [(i, (i + step) % size) for i in range(size)])  52.4 us
    pallas_call x3, Pallas kernels, place(): pl.pallas_call(functools.partial(_place_kernel, src_blocks, dst_blocks, t...  36.7 us
    dot_general x1, matrix products, on_device(): jnp.dot(left_dense, right_dense, preferred_element_type=jnp.float32)  12.8 us
    ppermute x5, starting transfers between devices, ring_shift(): return lax.ppermute(x, axis, [(i, (i + step) % size) for i in range(size)])  7.66 us
  transfers between devices with their start and end apart: 7, of which 4 were waited for; matrix products, arithmetic and copies ran while one was open for 6% of the time, Pallas kernels for 2%

profile of v2, /device:TPU:32, one launch (start us, length us, event | category | flops | bytes accessed | tf_op | source)
XLA Modules:
  0.0 256.7 jit_solution(12493035183296740857)
XLA Ops:
  6.5 1.4 fusion.6
  9.2 2.1 select_bitcast_fusion.1
  11.3 2.6 %pad_maximum_fusion = bf16[2,3072,384]{2,1,0:T(8,128)(2,1)} fusion(bf16[1,3072,384]{2,1,0:T(8,128)(2,1)S(1)} %get-tuple-element.11, bf16[1,3072,384]{2,1,0:T(8,128)(2,1)S(1)} %get-tuple-element.10), kind=kLoop, calls=%fused_computation.1 | loop fusion | flops 2359296 | bytes 9437184 | tf_op jit(solution)/shard_map/stack | solution.py:122
  14.0 104.1 %reduce-scatter.2.cloned.1.call-done = bf16[192,384]{1,0:T(8,128)(2,1)} async-done(((bf16[6144,384]{1,0:T(8,128)(2,1)}), bf16[192,384]{1,0:T(8,128)(2,1)}) %reduce-scatter.2.cloned.1.call-update) | async-done | bytes 147472 | tf_op jit(solution)/shard_map/reduce_scatter | solution.py:123
  123.4 0.2 select_bitcast_fusion.3
  123.6 0.1 pad_maximum_fusion.1
  123.8 1.8 collective-permute-start
  125.6 0.6 broadcast_compare_fusion
  126.2 28.6 %collective-permute-done = bf16[2,768,384]{2,1,0:T(8,128)(2,1)S(1)} collective-permute-done((bf16[2,768,384]{2,1,0:T(8,128)(2,1)S(1)}, bf16[2,768,384]{2,1,0:T(8,128)(2,1)S(1)}, u32[]{:S(2)}, u32[]{:S(2)}) %collective-permute-start) | collective-permute-done | bytes 1179680 | tf_op jit(solution)/shard_map/ppermute | solution.py:81
  154.7 0.2 broadcast_select_fusion
  155.0 1.7 collective-permute-start.1
  156.7 1.6 collective-permute-start.2
  158.3 23.3 %collective-permute-done.1 = bf16[2,768,384]{2,1,0:T(8,128)(2,1)S(1)} collective-permute-done((bf16[2,768,384]{2,1,0:T(8,128)(2,1)S(1)}, bf16[2,768,384]{2,1,0:T(8,128)(2,1)S(1)}, u32[]{:S(2)}, u32[]{:S(2)}) %collective-permute-start.1) | collective-permute-done | bytes 1179680 | tf_op jit(solution)/shard_map/ppermute | solution.py:81
  181.6 0.6 collective-permute-done.2
  182.2 0.3 select_select_fusion
  182.5 0.1 fusion.5
  182.6 2.5 collective-permute-start.4
  187.7 0.9 dynamic-slice_subtract_fusion.3
  188.6 0.7 copy.6
  189.3 1.5 reshape.28.table
  190.8 0.7 copy.8
  191.5 1.4 reshape.30
  192.9 0.7 copy.7
  193.6 1.4 reshape.29
  195.0 0.9 dynamic-slice_subtract_fusion.1
  196.2 0.7 pad_add_fusion.1.table
  196.9 1.3 pad_add_fusion.table
  198.2 2.1 maximum_select_fusion.values
  200.3 6.3 %shard_map.38 = bf16[1536,768]{1,0:T(8,128)(2,1)} custom-call(s32[144]{0:T(256)} %pad_add_fusion.1.table, bf16[2,768,384]{2,1,0:T(8,128)(2,1)} %maximum_select_fusion.values), custom_call_target="tpu_custom_call" | custom-call | tf_op jit(solution)/shard_map/pallas_call | solution.py:68
  206.7 19.9 %shard_map.37 = bf16[3072,1536]{1,0:T(8,128)(2,1)} custom-call(s32[576]{0:T(1024)} %pad_add_fusion.table, bf16[2,3072,384]{2,1,0:T(8,128)(2,1)} %bitcast.17), custom_call_target="tpu_custom_call" | custom-call | tf_op jit(solution)/shard_map/pallas_call | solution.py:68
  226.5 12.8 %fusion.values = bf16[1,3072,768]{2,1,0:T(8,128)(2,1)} fusion(bf16[3072,1536]{1,0:T(8,128)(2,1)} %shard_map.37, bf16[1536,768]{1,0:T(8,128)(2,1)S(1)} %copy-done.1), kind=kOutput, calls=%fused_computation.2 | convolution fusion | flops 7250116608 | bytes 16515072 | tf_op jit(solution)/shard_map/dot_general | solution.py:142
  239.3 10.6 %shard_map.39 = bf16[3072,384]{1,0:T(8,128)(2,1)} custom-call(s32[288]{0:T(512)} %reshape.28.table, bf16[1,3072,768]{2,1,0:T(8,128)(2,1)} %fusion.values), custom_call_target="tpu_custom_call" | custom-call | tf_op jit(solution)/shard_map/pallas_call | solution.py:68
  (20 shorter events, 0.5 us)
Async XLA Ops:
  6.5 111.6 %reduce-scatter.2.cloned.1.call-start = ((), (), s32[]{:S(2)}) async-start(), calls=%async_computation.1 | async-start | bytes 4866048 | tf_op jit(solution)/shard_map/reduce_scatter | solution.py:123
  13.9 109.4 %copy-start = (bf16[3072,384]{1,0:T(8,128)(2,1)S(1)}, bf16[3072,384]{1,0:T(8,128)(2,1)}, u32[]{:S(2)}) copy-start(bf16[3072,384]{1,0:T(8,128)(2,1)} %param.3) | copy-start | bytes 7077892
  14.0 192.7 %all-gather.2.cloned.1.call-start = ((), (), s32[]{:S(2)}) async-start(), calls=%async_computation.2 | async-start | bytes 4866048 | tf_op jit(solution)/shard_map/all_gather | solution.py:124
  123.6 2.0 copy-start.2
  123.8 31.0 %collective-permute-start = (bf16[2,768,384]{2,1,0:T(8,128)(2,1)S(1)}, bf16[2,768,384]{2,1,0:T(8,128)(2,1)S(1)}, u32[]{:S(2)}, u32[]{:S(2)}) collective-permute-start(bf16[2,768,384]{2,1,0:T(8,128)(2,1)S(1)} %pad_maximum_fusion.1), channel_id=1, source_target_pairs={{0,128},{128,0},{1,129},{129,1},{2,130},{130,2},{3,131},{131,3},{4... | collective-permute-start | bytes 3538952 | tf_op jit(solution)/shard_map/ppermute | solution.py:81
  155.0 26.6 %collective-permute-start.1 = (bf16[2,768,384]{2,1,0:T(8,128)(2,1)S(1)}, bf16[2,768,384]{2,1,0:T(8,128)(2,1)S(1)}, u32[]{:S(2)}, u32[]{:S(2)}) collective-permute-start(bf16[2,768,384]{2,1,0:T(8,128)(2,1)S(1)} %broadcast_select_fusion), channel_id=1, source_target_pairs={{0,32},{32,64},{64,96},{96,0},{1,33},{33,65},{65,97},{97,1},{2,34}... | collective-permute-start | bytes 3538952 | tf_op jit(solution)/shard_map/ppermute | solution.py:81
  156.7 25.5 %collective-permute-start.2 = (bf16[2,768,384]{2,1,0:T(8,128)(2,1)S(1)}, bf16[2,768,384]{2,1,0:T(8,128)(2,1)S(1)}, u32[]{:S(2)}, u32[]{:S(2)}) collective-permute-start(bf16[2,768,384]{2,1,0:T(8,128)(2,1)S(1)} %broadcast_select_fusion), channel_id=1, source_target_pairs={{0,96},{32,0},{64,32},{96,64},{1,97},{33,1},{65,33},{97,65},{2,98}... | collective-permute-start | bytes 3538952 | tf_op jit(solution)/shard_map/ppermute | solution.py:81
  182.6 15.6 %collective-permute-start.4 = (bf16[2,384,384]{2,1,0:T(8,128)(2,1)S(1)}, bf16[2,384,384]{2,1,0:T(8,128)(2,1)S(1)}, u32[]{:S(2)}, u32[]{:S(2)}) collective-permute-start(bf16[2,384,384]{2,1,0:T(8,128)(2,1)S(1)} %get-tuple-element.13), channel_id=1, source_target_pairs={{0,96},{32,0},{64,32},{96,64},{1,97},{33,1},{65,33},{97,65},{2,98}... | collective-permute-start | bytes 1769480 | tf_op jit(solution)/shard_map/ppermute | solution.py:81
  185.1 13.1 %collective-permute-start.3 = (bf16[2,384,384]{2,1,0:T(8,128)(2,1)S(1)}, bf16[2,384,384]{2,1,0:T(8,128)(2,1)S(1)}, u32[]{:S(2)}, u32[]{:S(2)}) collective-permute-start(bf16[2,384,384]{2,1,0:T(8,128)(2,1)S(1)} %get-tuple-element.12), channel_id=1, source_target_pairs={{0,32},{32,64},{64,96},{96,0},{1,33},{33,65},{65,97},{97,1},{2,34}... | collective-permute-start | bytes 1769480 | tf_op jit(solution)/shard_map/ppermute | solution.py:81
  206.7 19.9 %copy-start.1 = (bf16[1536,768]{1,0:T(8,128)(2,1)S(1)}, bf16[1536,768]{1,0:T(8,128)(2,1)}, u32[]{:S(2)}) copy-start(bf16[1536,768]{1,0:T(8,128)(2,1)} %shard_map.38) | copy-start | bytes 7077892
Sparse Core Ops, SparseCore 0:
  14.1 104.0 reduce-scatter.1
  120.7 61.5 all-gather.1

commit v3 on v2

--- a/solution.py
+++ b/solution.py
@@ -121,12 +121,13 @@
 
     stacked = jnp.stack(lefts).reshape(2 * density.shape[0], density.shape[1])
     part = lax.psum_scatter(stacked, COL_AXES, scatter_dimension=0, tiled=True)
-    left_all = lax.all_gather(part, COL_AXES, axis=0, tiled=True).reshape(2, *density.shape)
 
     band_all = jnp.stack(bands)
     owner_row = panels // panels_per_row
     n_ry = lax.axis_size("ry")
     band_all = row_broadcast(band_all, owner_row // n_ry, owner_row % n_ry)
+    part, band_all = lax.optimization_barrier((part, band_all))
+    left_all = lax.all_gather(part, COL_AXES, axis=0, tiled=True).reshape(2, *density.shape)
 
     left_tables = []
     right_tables = []

time: 260 us -> 235 us (0.904)
  waiting for transfers between devices: 157 us -> 137 us
  local copies, waits for them, and re-layouts: 8.28 us -> 3.12 us
    reduce_scatter x1, waiting for transfers between devices: 104 us -> 22.6 us  [on_device(): part = lax.psum_scatter(stacked, COL_AXES, scatter_dimension=0, tiled=True)]
    all_gather x1, waiting for transfers between devices: 0.01 us -> 49.3 us  [on_device(): lax.all_gather(part, COL_AXES, axis=0, tiled=True)]
    ppermute x5, waiting for transfers between devices: 52.4 us -> 65 us  [ring_shift(): return lax.ppermute(x, axis, [(i, (i + step) % size) for i in range(size)])]
    reshape x2, local copies, waits for them, and re-layouts: 2.86 us -> 0.24 us  [on_device(): left_tables.append(group_cols.reshape(-1))]
  transfers between devices with their start and end apart: 7 -> 7, of which waited for: 4 -> 6; matrix products, arithmetic and copies ran while one was open for 6% -> 3% of each run, Pallas kernels for 2% -> 3%
where the time goes in v3:
time: 235 us; the launch traced here: 231 us
  waiting for transfers between devices  137 us (58%)
  Pallas kernels  36.7 us (16%)
  between operations  23.1 us (10%)
  matrix products  12.8 us (5%)
  other arithmetic  10.3 us (4%)
  starting transfers between devices  8.36 us (4%)
  local copies, waits for them, and re-layouts  3.12 us (1%)
    ppermute x5, waiting for transfers between devices, ring_shift(): return lax.ppermute(x, axis, [(i, (i + step) % size) for i in range(size)])  65 us
    all_gather x1, waiting for transfers between devices, on_device(): lax.all_gather(part, COL_AXES, axis=0, tiled=True)  49.3 us
    pallas_call x3, Pallas kernels, place(): pl.pallas_call(functools.partial(_place_kernel, src_blocks, dst_blocks, t...  36.7 us
    reduce_scatter x1, waiting for transfers between devices, on_device(): part = lax.psum_scatter(stacked, COL_AXES, scatter_dimension=0, tiled=True)  22.6 us
    dot_general x1, matrix products, on_device(): jnp.dot(left_dense, right_dense, preferred_element_type=jnp.float32)  12.8 us
    ppermute x5, starting transfers between devices, ring_shift(): return lax.ppermute(x, axis, [(i, (i + step) % size) for i in range(size)])  8.31 us
    another operation x2, other arithmetic, on_device(): stacked = jnp.stack(lefts).reshape(2 * density.shape[0], density.shape[1])  4.73 us
  transfers between devices with their start and end apart: 7, of which 6 were waited for; matrix products, arithmetic and copies ran while one was open for 3% of the time, Pallas kernels for 3%

profile of v3, /device:TPU:32, one launch (start us, length us, event | category | flops | bytes accessed | tf_op | source)
XLA Modules:
  0.0 231.2 jit_solution(5310965264229542977)
XLA Ops:
  6.5 1.4 fusion.6
  9.3 2.1 select_bitcast_fusion.1
  11.4 2.6 %pad_maximum_fusion = bf16[2,3072,384]{2,1,0:T(8,128)(2,1)} fusion(bf16[1,3072,384]{2,1,0:T(8,128)(2,1)S(1)} %get-tuple-element.15, bf16[1,3072,384]{2,1,0:T(8,128)(2,1)S(1)} %get-tuple-element.14), kind=kLoop, calls=%fused_computation.1 | loop fusion | flops 2359296 | bytes 9437184 | tf_op jit(solution)/shard_map/stack | solution.py:122
  19.6 0.2 select_bitcast_fusion.3
  19.9 0.1 pad_maximum_fusion.1
  20.0 1.9 collective-permute-start
  22.0 25.8 %collective-permute-done = bf16[2,768,384]{2,1,0:T(8,128)(2,1)S(1)} collective-permute-done((bf16[2,768,384]{2,1,0:T(8,128)(2,1)S(1)}, bf16[2,768,384]{2,1,0:T(8,128)(2,1)S(1)}, u32[]{:S(2)}, u32[]{:S(2)}) %collective-permute-start) | collective-permute-done | bytes 1179680 | tf_op jit(solution)/shard_map/ppermute | solution.py:81
  47.8 0.2 broadcast_select_fusion
  48.1 1.7 collective-permute-start.1
  49.7 1.7 collective-permute-start.2
  51.4 24.9 %collective-permute-done.1 = bf16[2,768,384]{2,1,0:T(8,128)(2,1)S(1)} collective-permute-done((bf16[2,768,384]{2,1,0:T(8,128)(2,1)S(1)}, bf16[2,768,384]{2,1,0:T(8,128)(2,1)S(1)}, u32[]{:S(2)}, u32[]{:S(2)}) %collective-permute-start.1) | collective-permute-done | bytes 1179680 | tf_op jit(solution)/shard_map/ppermute | solution.py:81
  76.3 0.3 select_select_fusion
  76.6 0.1 fusion.5
  76.7 3.1 %collective-permute-start.4 = (bf16[2,384,384]{2,1,0:T(8,128)(2,1)S(1)}, bf16[2,384,384]{2,1,0:T(8,128)(2,1)S(1)}, u32[]{:S(2)}, u32[]{:S(2)}) collective-permute-start(bf16[2,384,384]{2,1,0:T(8,128)(2,1)S(1)} %get-tuple-element.17), channel_id=1, source_target_pairs={{0,96},{32,0},{64,32},{96,64},{1,97},{33,1},{65,33},{97,65},{2,98}... | collective-permute-start | bytes 1769480 | tf_op jit(solution)/shard_map/ppermute | solution.py:81
  79.8 10.8 %collective-permute-done.4 = bf16[2,384,384]{2,1,0:T(8,128)(2,1)S(1)} collective-permute-done((bf16[2,384,384]{2,1,0:T(8,128)(2,1)S(1)}, bf16[2,384,384]{2,1,0:T(8,128)(2,1)S(1)}, u32[]{:S(2)}, u32[]{:S(2)}) %collective-permute-start.4) | collective-permute-done | bytes 589856 | tf_op jit(solution)/shard_map/ppermute | solution.py:81
  90.7 3.4 %collective-permute-done.3 = bf16[2,384,384]{2,1,0:T(8,128)(2,1)S(1)} collective-permute-done((bf16[2,384,384]{2,1,0:T(8,128)(2,1)S(1)}, bf16[2,384,384]{2,1,0:T(8,128)(2,1)S(1)}, u32[]{:S(2)}, u32[]{:S(2)}) %collective-permute-start.3) | collective-permute-done | bytes 589856 | tf_op jit(solution)/shard_map/ppermute | solution.py:81
  94.1 1.5 maximum_select_fusion.values
  95.6 22.6 %reduce-scatter.2.cloned.1.call-done = bf16[192,384]{1,0:T(8,128)(2,1)} async-done(((bf16[6144,384]{1,0:T(8,128)(2,1)}), bf16[192,384]{1,0:T(8,128)(2,1)}) %reduce-scatter.2.cloned.1.call-update) | async-done | bytes 147472 | tf_op jit(solution)/shard_map/reduce_scatter | solution.py:123
  120.9 0.8 dynamic-slice_subtract_fusion.3
  121.9 0.7 reshape.28.table
  122.7 0.1 reshape.30
  122.9 0.1 reshape.29
  123.0 0.9 dynamic-slice_subtract_fusion.1
  123.9 0.1 copy.10
  124.1 0.1 copy.9
  124.3 0.7 pad_add_fusion.1.table
  125.0 0.6 pad_add_fusion.table
  125.6 6.3 %shard_map.38 = bf16[1536,768]{1,0:T(8,128)(2,1)} custom-call(s32[144]{0:T(256)} %pad_add_fusion.1.table, bf16[2,768,384]{2,1,0:T(8,128)(2,1)} %maximum_select_fusion.values), custom_call_target="tpu_custom_call" | custom-call | tf_op jit(solution)/shard_map/pallas_call | solution.py:68
  131.9 49.3 %all-gather.2.cloned.1.call-done = bf16[6144,384]{1,0:T(8,128)(2,1)} async-done(((bf16[192,384]{1,0:T(8,128)(2,1)}), bf16[6144,384]{1,0:T(8,128)(2,1)}) %all-gather.2.cloned.1.call-update) | async-done | bytes 4718608 | tf_op jit(solution)/shard_map/all_gather | solution.py:130
  181.2 19.9 %shard_map.37 = bf16[3072,1536]{1,0:T(8,128)(2,1)} custom-call(s32[576]{0:T(1024)} %pad_add_fusion.table, bf16[2,3072,384]{2,1,0:T(8,128)(2,1)} %bitcast.17), custom_call_target="tpu_custom_call" | custom-call | tf_op jit(solution)/shard_map/pallas_call | solution.py:68
  201.1 12.8 %fusion.values = bf16[1,3072,768]{2,1,0:T(8,128)(2,1)} fusion(bf16[3072,1536]{1,0:T(8,128)(2,1)} %shard_map.37, bf16[1536,768]{1,0:T(8,128)(2,1)S(1)} %copy-done.1), kind=kOutput, calls=%fused_computation.2 | convolution fusion | flops 7250116608 | bytes 16515072 | tf_op jit(solution)/shard_map/dot_general | solution.py:143
  213.9 10.6 %shard_map.39 = bf16[3072,384]{1,0:T(8,128)(2,1)} custom-call(s32[288]{0:T(512)} %reshape.28.table, bf16[1,3072,768]{2,1,0:T(8,128)(2,1)} %fusion.values), custom_call_target="tpu_custom_call" | custom-call | tf_op jit(solution)/shard_map/pallas_call | solution.py:68
  (20 shorter events, 0.6 us)
Async XLA Ops:
  6.5 111.7 %reduce-scatter.2.cloned.1.call-start = ((), (), s32[]{:S(2)}) async-start(), calls=%async_computation.1 | async-start | bytes 4866048 | tf_op jit(solution)/shard_map/reduce_scatter | solution.py:123
  14.0 5.6 %copy-start = (bf16[3072,384]{1,0:T(8,128)(2,1)S(1)}, bf16[3072,384]{1,0:T(8,128)(2,1)}, u32[]{:S(2)}) copy-start(bf16[3072,384]{1,0:T(8,128)(2,1)} %param.3) | copy-start | bytes 7077892
  14.0 167.2 %all-gather.2.cloned.1.call-start = ((), (), s32[]{:S(2)}) async-start(), calls=%async_computation.2 | async-start | bytes 4866048 | tf_op jit(solution)/shard_map/all_gather | solution.py:130
  19.9 2.1 copy-start.2
  20.0 27.8 %collective-permute-start = (bf16[2,768,384]{2,1,0:T(8,128)(2,1)S(1)}, bf16[2,768,384]{2,1,0:T(8,128)(2,1)S(1)}, u32[]{:S(2)}, u32[]{:S(2)}) collective-permute-start(bf16[2,768,384]{2,1,0:T(8,128)(2,1)S(1)} %pad_maximum_fusion.1), channel_id=1, source_target_pairs={{0,128},{128,0},{1,129},{129,1},{2,130},{130,2},{3,131},{131,3},{4... | collective-permute-start | bytes 3538952 | tf_op jit(solution)/shard_map/ppermute | solution.py:81
  48.1 28.2 %collective-permute-start.1 = (bf16[2,768,384]{2,1,0:T(8,128)(2,1)S(1)}, bf16[2,768,384]{2,1,0:T(8,128)(2,1)S(1)}, u32[]{:S(2)}, u32[]{:S(2)}) collective-permute-start(bf16[2,768,384]{2,1,0:T(8,128)(2,1)S(1)} %broadcast_select_fusion), channel_id=1, source_target_pairs={{0,32},{32,64},{64,96},{96,0},{1,33},{33,65},{65,97},{97,1},{2,34}... | collective-permute-start | bytes 3538952 | tf_op jit(solution)/shard_map/ppermute | solution.py:81
  49.7 26.6 %collective-permute-start.2 = (bf16[2,768,384]{2,1,0:T(8,128)(2,1)S(1)}, bf16[2,768,384]{2,1,0:T(8,128)(2,1)S(1)}, u32[]{:S(2)}, u32[]{:S(2)}) collective-permute-start(bf16[2,768,384]{2,1,0:T(8,128)(2,1)S(1)} %broadcast_select_fusion), channel_id=1, source_target_pairs={{0,96},{32,0},{64,32},{96,64},{1,97},{33,1},{65,33},{97,65},{2,98}... | collective-permute-start | bytes 3538952 | tf_op jit(solution)/shard_map/ppermute | solution.py:81
  76.7 13.9 %collective-permute-start.4 = (bf16[2,384,384]{2,1,0:T(8,128)(2,1)S(1)}, bf16[2,384,384]{2,1,0:T(8,128)(2,1)S(1)}, u32[]{:S(2)}, u32[]{:S(2)}) collective-permute-start(bf16[2,384,384]{2,1,0:T(8,128)(2,1)S(1)} %get-tuple-element.17), channel_id=1, source_target_pairs={{0,96},{32,0},{64,32},{96,64},{1,97},{33,1},{65,33},{97,65},{2,98}... | collective-permute-start | bytes 1769480 | tf_op jit(solution)/shard_map/ppermute | solution.py:81
  79.8 14.3 %collective-permute-start.3 = (bf16[2,384,384]{2,1,0:T(8,128)(2,1)S(1)}, bf16[2,384,384]{2,1,0:T(8,128)(2,1)S(1)}, u32[]{:S(2)}, u32[]{:S(2)}) collective-permute-start(bf16[2,384,384]{2,1,0:T(8,128)(2,1)S(1)} %get-tuple-element.16), channel_id=1, source_target_pairs={{0,32},{32,64},{64,96},{96,0},{1,33},{33,65},{65,97},{97,1},{2,34}... | collective-permute-start | bytes 1769480 | tf_op jit(solution)/shard_map/ppermute | solution.py:81
  181.2 19.9 %copy-start.1 = (bf16[1536,768]{1,0:T(8,128)(2,1)S(1)}, bf16[1536,768]{1,0:T(8,128)(2,1)}, u32[]{:S(2)}) copy-start(bf16[1536,768]{1,0:T(8,128)(2,1)} %shard_map.38) | copy-start | bytes 7077892
Sparse Core Ops, SparseCore 0:
  14.1 104.0 reduce-scatter.1
  120.7 60.3 all-gather.1

commit v4 on v3

--- a/solution.py
+++ b/solution.py
@@ -15,8 +15,7 @@
 
 
 def _halves(chunk):
-    wide = chunk.astype(jnp.float32)
-    return wide, pltpu.roll(wide, BLK, 1)
+    return chunk, pltpu.roll(chunk, BLK, 1)
 
 
 def _place_kernel(src_blocks, dst_blocks, tile_rows, block_rows, table, values, out):
@@ -28,9 +27,10 @@
     placing = src_blocks < dst_blocks
     entries = src_blocks if placing else dst_blocks
     per_step = block_rows * entries
-    for q in range(tile_rows // BLK):
+
+    def one_row(q, carry):
         base = step * per_step + (tile * (tile_rows // BLK) + q) * entries
-        rows = pl.ds(q * BLK, BLK)
+        rows = pl.ds(pl.multiple_of(q * BLK, BLK), BLK)
         plain = []
         swapped = []
         for c in range(src_blocks // 2):
@@ -46,14 +46,17 @@
             else:
                 sources.append(jnp.where(high, own, other))
         for p in range(dst_blocks // 2):
-            acc = jnp.zeros((BLK, 2 * BLK), jnp.float32)
+            acc = jnp.zeros((BLK, 2 * BLK), out.dtype)
             for t in range(src_blocks):
                 if placing:
                     hit = half + 2 * p == table[base + t]
                 else:
                     hit = jnp.where(high, table[base + 2 * p + 1], table[base + 2 * p]) == t
                 acc = jnp.where(hit, sources[t], acc)
-            out[rows, pl.ds(p * 2 * BLK, 2 * BLK)] = acc.astype(out.dtype)
+            out[rows, pl.ds(p * 2 * BLK, 2 * BLK)] = acc
+        return carry
+
+    lax.fori_loop(0, tile_rows // BLK, one_row, 0)
 
 
 def place(values, table, src_blocks, dst_blocks, tile_rows, by_rows):
@@ -138,10 +141,10 @@
         band_rows = lax.dynamic_slice_in_dim(neighbours, number * CB, CB, 0)
         band_cols = lax.dynamic_slice_in_dim(band_rows, col_index * slot_count, slot_count, 1) - col_index * CB
         right_tables.append(band_cols.reshape(-1))
-    left_dense = place(left_all, jnp.concatenate(left_tables), slot_count, CB, 256, False)
-    right_dense = place(band_all, jnp.concatenate(right_tables), slot_count, CB, 256, True)
+    left_dense = place(left_all, jnp.concatenate(left_tables), slot_count, CB, 1536, False)
+    right_dense = place(band_all, jnp.concatenate(right_tables), slot_count, CB, 768, True)
     product = jnp.dot(left_dense, right_dense, preferred_element_type=jnp.float32).astype(jnp.bfloat16)
-    return place(product[None], own_cols.reshape(-1), CB, slot_count, 256, True)
+    return place(product[None], own_cols.reshape(-1), CB, slot_count, 768, True)
 
 
 def solution(mesh):

time: 235 us -> 231 us (0.983)
  Pallas kernels: 36.7 us -> 34.1 us
    pallas_call x3, Pallas kernels: 36.7 us -> 34.1 us  [place(): pl.pallas_call(functools.partial(_place_kernel, src_blocks, dst_blocks, t...]
where the time goes in v4:
time: 231 us; the launch traced here: 229 us
  waiting for transfers between devices  137 us (59%)
  Pallas kernels  34.1 us (15%)
  between operations  23.1 us (10%)
  matrix products  12.8 us (6%)
  other arithmetic  10.2 us (4%)
  starting transfers between devices  8.36 us (4%)
  local copies, waits for them, and re-layouts  3.12 us (1%)
    ppermute x5, waiting for transfers between devices, ring_shift(): return lax.ppermute(x, axis, [(i, (i + step) % size) for i in range(size)])  65 us
    all_gather x1, waiting for transfers between devices, on_device(): lax.all_gather(part, COL_AXES, axis=0, tiled=True)  49.3 us
    pallas_call x3, Pallas kernels, place(): pl.pallas_call(functools.partial(_place_kernel, src_blocks, dst_blocks, t...  34.1 us
    reduce_scatter x1, waiting for transfers between devices, on_device(): part = lax.psum_scatter(stacked, COL_AXES, scatter_dimension=0, tiled=True)  22.6 us
    dot_general x1, matrix products, on_device(): jnp.dot(left_dense, right_dense, preferred_element_type=jnp.float32)  12.8 us
    ppermute x5, starting transfers between devices, ring_shift(): return lax.ppermute(x, axis, [(i, (i + step) % size) for i in range(size)])  8.31 us
    another operation x2, other arithmetic, on_device(): stacked = jnp.stack(lefts).reshape(2 * density.shape[0], density.shape[1])  4.73 us
  transfers between devices with their start and end apart: 7, of which 6 were waited for; matrix products, arithmetic and copies ran while one was open for 3% of the time, Pallas kernels for 3%

profile of v4, /device:TPU:32, one launch (start us, length us, event | category | flops | bytes accessed | tf_op | source)
XLA Modules:
  0.0 228.6 jit_solution(13479915252069939406)
XLA Ops:
  6.5 1.4 fusion.6
  9.3 2.1 select_bitcast_fusion.1
  11.4 2.6 %pad_maximum_fusion = bf16[2,3072,384]{2,1,0:T(8,128)(2,1)} fusion(bf16[1,3072,384]{2,1,0:T(8,128)(2,1)S(1)} %get-tuple-element.15, bf16[1,3072,384]{2,1,0:T(8,128)(2,1)S(1)} %get-tuple-element.14), kind=kLoop, calls=%fused_computation.1 | loop fusion | flops 2359296 | bytes 9437184 | tf_op jit(solution)/shard_map/stack | solution.py:125
  19.6 0.2 select_bitcast_fusion.3
  19.9 0.1 pad_maximum_fusion.1
  20.0 1.9 collective-permute-start
  22.0 25.8 %collective-permute-done = bf16[2,768,384]{2,1,0:T(8,128)(2,1)S(1)} collective-permute-done((bf16[2,768,384]{2,1,0:T(8,128)(2,1)S(1)}, bf16[2,768,384]{2,1,0:T(8,128)(2,1)S(1)}, u32[]{:S(2)}, u32[]{:S(2)}) %collective-permute-start) | collective-permute-done | bytes 1179680 | tf_op jit(solution)/shard_map/ppermute | solution.py:84
  47.8 0.2 broadcast_select_fusion
  48.1 1.7 collective-permute-start.1
  49.7 1.7 collective-permute-start.2
  51.4 24.9 %collective-permute-done.1 = bf16[2,768,384]{2,1,0:T(8,128)(2,1)S(1)} collective-permute-done((bf16[2,768,384]{2,1,0:T(8,128)(2,1)S(1)}, bf16[2,768,384]{2,1,0:T(8,128)(2,1)S(1)}, u32[]{:S(2)}, u32[]{:S(2)}) %collective-permute-start.1) | collective-permute-done | bytes 1179680 | tf_op jit(solution)/shard_map/ppermute | solution.py:84
  76.3 0.3 select_select_fusion
  76.6 0.1 fusion.5
  76.7 3.1 %collective-permute-start.4 = (bf16[2,384,384]{2,1,0:T(8,128)(2,1)S(1)}, bf16[2,384,384]{2,1,0:T(8,128)(2,1)S(1)}, u32[]{:S(2)}, u32[]{:S(2)}) collective-permute-start(bf16[2,384,384]{2,1,0:T(8,128)(2,1)S(1)} %get-tuple-element.17), channel_id=1, source_target_pairs={{0,96},{32,0},{64,32},{96,64},{1,97},{33,1},{65,33},{97,65},{2,98}... | collective-permute-start | bytes 1769480 | tf_op jit(solution)/shard_map/ppermute | solution.py:84
  79.8 10.8 %collective-permute-done.4 = bf16[2,384,384]{2,1,0:T(8,128)(2,1)S(1)} collective-permute-done((bf16[2,384,384]{2,1,0:T(8,128)(2,1)S(1)}, bf16[2,384,384]{2,1,0:T(8,128)(2,1)S(1)}, u32[]{:S(2)}, u32[]{:S(2)}) %collective-permute-start.4) | collective-permute-done | bytes 589856 | tf_op jit(solution)/shard_map/ppermute | solution.py:84
  90.7 3.4 %collective-permute-done.3 = bf16[2,384,384]{2,1,0:T(8,128)(2,1)S(1)} collective-permute-done((bf16[2,384,384]{2,1,0:T(8,128)(2,1)S(1)}, bf16[2,384,384]{2,1,0:T(8,128)(2,1)S(1)}, u32[]{:S(2)}, u32[]{:S(2)}) %collective-permute-start.3) | collective-permute-done | bytes 589856 | tf_op jit(solution)/shard_map/ppermute | solution.py:84
  94.1 1.5 maximum_select_fusion.values
  95.6 22.6 %reduce-scatter.2.cloned.1.call-done = bf16[192,384]{1,0:T(8,128)(2,1)} async-done(((bf16[6144,384]{1,0:T(8,128)(2,1)}), bf16[192,384]{1,0:T(8,128)(2,1)}) %reduce-scatter.2.cloned.1.call-update) | async-done | bytes 147472 | tf_op jit(solution)/shard_map/reduce_scatter | solution.py:126
  120.9 0.8 dynamic-slice_subtract_fusion.3
  121.9 0.7 reshape.28.table
  122.7 0.1 reshape.30
  122.9 0.1 reshape.29
  123.0 0.8 dynamic-slice_subtract_fusion.1
  123.9 0.1 copy.10
  124.0 0.1 copy.9
  124.2 0.7 pad_add_fusion.1.table
  124.9 0.6 pad_add_fusion.table
  125.5 6.3 %shard_map.38 = bf16[1536,768]{1,0:T(8,128)(2,1)} custom-call(s32[144]{0:T(256)} %pad_add_fusion.1.table, bf16[2,768,384]{2,1,0:T(8,128)(2,1)} %maximum_select_fusion.values), custom_call_target="tpu_custom_call" | custom-call | tf_op jit(solution)/shard_map/pallas_call | solution.py:71
  131.9 49.3 %all-gather.2.cloned.1.call-done = bf16[6144,384]{1,0:T(8,128)(2,1)} async-done(((bf16[192,384]{1,0:T(8,128)(2,1)}), bf16[6144,384]{1,0:T(8,128)(2,1)}) %all-gather.2.cloned.1.call-update) | async-done | bytes 4718608 | tf_op jit(solution)/shard_map/all_gather | solution.py:133
  181.2 17.8 %shard_map.37 = bf16[3072,1536]{1,0:T(8,128)(2,1)} custom-call(s32[576]{0:T(1024)} %pad_add_fusion.table, bf16[2,3072,384]{2,1,0:T(8,128)(2,1)} %bitcast.17), custom_call_target="tpu_custom_call" | custom-call | tf_op jit(solution)/shard_map/pallas_call | solution.py:71
  199.0 12.8 %fusion.values = bf16[1,3072,768]{2,1,0:T(8,128)(2,1)} fusion(bf16[3072,1536]{1,0:T(8,128)(2,1)} %shard_map.37, bf16[1536,768]{1,0:T(8,128)(2,1)S(1)} %copy-done.1), kind=kOutput, calls=%fused_computation.2 | convolution fusion | flops 7250116608 | bytes 16515072 | tf_op jit(solution)/shard_map/dot_general | solution.py:146
  211.7 10.0 %shard_map.39 = bf16[3072,384]{1,0:T(8,128)(2,1)} custom-call(s32[288]{0:T(512)} %reshape.28.table, bf16[1,3072,768]{2,1,0:T(8,128)(2,1)} %fusion.values), custom_call_target="tpu_custom_call" | custom-call | tf_op jit(solution)/shard_map/pallas_call | solution.py:71
  (20 shorter events, 0.6 us)
Async XLA Ops:
  6.5 111.7 %reduce-scatter.2.cloned.1.call-start = ((), (), s32[]{:S(2)}) async-start(), calls=%async_computation.1 | async-start | bytes 4866048 | tf_op jit(solution)/shard_map/reduce_scatter | solution.py:126
  14.0 5.6 %copy-start = (bf16[3072,384]{1,0:T(8,128)(2,1)S(1)}, bf16[3072,384]{1,0:T(8,128)(2,1)}, u32[]{:S(2)}) copy-start(bf16[3072,384]{1,0:T(8,128)(2,1)} %param.3) | copy-start | bytes 7077892
  14.0 167.2 %all-gather.2.cloned.1.call-start = ((), (), s32[]{:S(2)}) async-start(), calls=%async_computation.2 | async-start | bytes 4866048 | tf_op jit(solution)/shard_map/all_gather | solution.py:133
  19.9 2.1 copy-start.2
  20.0 27.8 %collective-permute-start = (bf16[2,768,384]{2,1,0:T(8,128)(2,1)S(1)}, bf16[2,768,384]{2,1,0:T(8,128)(2,1)S(1)}, u32[]{:S(2)}, u32[]{:S(2)}) collective-permute-start(bf16[2,768,384]{2,1,0:T(8,128)(2,1)S(1)} %pad_maximum_fusion.1), channel_id=1, source_target_pairs={{0,128},{128,0},{1,129},{129,1},{2,130},{130,2},{3,131},{131,3},{4... | collective-permute-start | bytes 3538952 | tf_op jit(solution)/shard_map/ppermute | solution.py:84
  48.1 28.2 %collective-permute-start.1 = (bf16[2,768,384]{2,1,0:T(8,128)(2,1)S(1)}, bf16[2,768,384]{2,1,0:T(8,128)(2,1)S(1)}, u32[]{:S(2)}, u32[]{:S(2)}) collective-permute-start(bf16[2,768,384]{2,1,0:T(8,128)(2,1)S(1)} %broadcast_select_fusion), channel_id=1, source_target_pairs={{0,32},{32,64},{64,96},{96,0},{1,33},{33,65},{65,97},{97,1},{2,34}... | collective-permute-start | bytes 3538952 | tf_op jit(solution)/shard_map/ppermute | solution.py:84
  49.7 26.6 %collective-permute-start.2 = (bf16[2,768,384]{2,1,0:T(8,128)(2,1)S(1)}, bf16[2,768,384]{2,1,0:T(8,128)(2,1)S(1)}, u32[]{:S(2)}, u32[]{:S(2)}) collective-permute-start(bf16[2,768,384]{2,1,0:T(8,128)(2,1)S(1)} %broadcast_select_fusion), channel_id=1, source_target_pairs={{0,96},{32,0},{64,32},{96,64},{1,97},{33,1},{65,33},{97,65},{2,98}... | collective-permute-start | bytes 3538952 | tf_op jit(solution)/shard_map/ppermute | solution.py:84
  76.7 13.9 %collective-permute-start.4 = (bf16[2,384,384]{2,1,0:T(8,128)(2,1)S(1)}, bf16[2,384,384]{2,1,0:T(8,128)(2,1)S(1)}, u32[]{:S(2)}, u32[]{:S(2)}) collective-permute-start(bf16[2,384,384]{2,1,0:T(8,128)(2,1)S(1)} %get-tuple-element.17), channel_id=1, source_target_pairs={{0,96},{32,0},{64,32},{96,64},{1,97},{33,1},{65,33},{97,65},{2,98}... | collective-permute-start | bytes 1769480 | tf_op jit(solution)/shard_map/ppermute | solution.py:84
  79.8 14.3 %collective-permute-start.3 = (bf16[2,384,384]{2,1,0:T(8,128)(2,1)S(1)}, bf16[2,384,384]{2,1,0:T(8,128)(2,1)S(1)}, u32[]{:S(2)}, u32[]{:S(2)}) collective-permute-start(bf16[2,384,384]{2,1,0:T(8,128)(2,1)S(1)} %get-tuple-element.16), channel_id=1, source_target_pairs={{0,32},{32,64},{64,96},{96,0},{1,33},{33,65},{65,97},{97,1},{2,34}... | collective-permute-start | bytes 1769480 | tf_op jit(solution)/shard_map/ppermute | solution.py:84
  181.2 17.8 %copy-start.1 = (bf16[1536,768]{1,0:T(8,128)(2,1)S(1)}, bf16[1536,768]{1,0:T(8,128)(2,1)}, u32[]{:S(2)}) copy-start(bf16[1536,768]{1,0:T(8,128)(2,1)} %shard_map.38) | copy-start | bytes 7077892
Sparse Core Ops, SparseCore 0:
  14.1 104.0 reduce-scatter.1
  120.7 60.4 all-gather.1

commit v5 on v4

--- a/solution.py
+++ b/solution.py
@@ -113,24 +113,26 @@
     my_rows = lax.dynamic_slice_in_dim(neighbours, row_index * row_blocks, row_blocks, 0)
     own_cols = lax.dynamic_slice_in_dim(my_rows, col_index * slot_count, slot_count, 1) - col_index * CB
 
-    lefts = []
+    core = lax.axis_index("cc")
+    panels = jnp.where(core == 0, panels, panels[::-1])
     bands = []
     for s in range(2):
         number = panels[s]
-        lefts.append(jnp.where(col_index == number, density, jnp.zeros_like(density)))
         offset = number % panels_per_row * CB * BLK
         band = lax.dynamic_slice_in_dim(density, offset, CB * BLK, 0)
         bands.append(jnp.where(row_index == number // panels_per_row, band, jnp.zeros_like(band)))
 
-    stacked = jnp.stack(lefts).reshape(2 * density.shape[0], density.shape[1])
-    part = lax.psum_scatter(stacked, COL_AXES, scatter_dimension=0, tiled=True)
+    handed = ring_shift(jnp.where(col_index == panels[1], density, jnp.zeros_like(density)), "cc", 2, 1)
+    carried = jnp.where(col_index == panels[0], density, handed)
+    part = lax.psum_scatter(carried, ("cx", "cz"), scatter_dimension=0, tiled=True)
 
     band_all = jnp.stack(bands)
     owner_row = panels // panels_per_row
     n_ry = lax.axis_size("ry")
     band_all = row_broadcast(band_all, owner_row // n_ry, owner_row % n_ry)
     part, band_all = lax.optimization_barrier((part, band_all))
-    left_all = lax.all_gather(part, COL_AXES, axis=0, tiled=True).reshape(2, *density.shape)
+    mine = lax.all_gather(part, ("cx", "cz"), axis=0, tiled=True)
+    other = ring_shift(mine, "cc", 2, 1)
 
     left_tables = []
     right_tables = []
@@ -141,9 +143,13 @@
         band_rows = lax.dynamic_slice_in_dim(neighbours, number * CB, CB, 0)
         band_cols = lax.dynamic_slice_in_dim(band_rows, col_index * slot_count, slot_count, 1) - col_index * CB
         right_tables.append(band_cols.reshape(-1))
-    left_dense = place(left_all, jnp.concatenate(left_tables), slot_count, CB, 1536, False)
     right_dense = place(band_all, jnp.concatenate(right_tables), slot_count, CB, 768, True)
-    product = jnp.dot(left_dense, right_dense, preferred_element_type=jnp.float32).astype(jnp.bfloat16)
+    first = place(mine[None], left_tables[0], slot_count, CB, 1536, False)
+    second = place(other[None], left_tables[1], slot_count, CB, 1536, False)
+    block = CB * BLK
+    product = jnp.dot(first, right_dense[:block], preferred_element_type=jnp.float32)
+    product = product + jnp.dot(second, right_dense[block:], preferred_element_type=jnp.float32)
+    product = product.astype(jnp.bfloat16)
     return place(product[None], own_cols.reshape(-1), CB, slot_count, 768, True)
 
 

time: 231 us -> 252 us (1.091)
  waiting for transfers between devices: 137 us -> 146 us
  matrix products: 12.8 us -> 18.9 us
  Pallas kernels: 34.1 us -> 37.5 us
    reduce_scatter x1, waiting for transfers between devices: 22.6 us -> 0.55 us  [on_device(): lax.psum_scatter(carried, ('cx', 'cz'), scatter_dimension=0, tiled=True)]
    all_gather x1, waiting for transfers between devices: 49.3 us -> 65.6 us  [on_device(): mine = lax.all_gather(part, ('cx', 'cz'), axis=0, tiled=True)]
    ppermute x5 -> x7, waiting for transfers between devices: 65 us -> 79.9 us  [ring_shift(): return lax.ppermute(x, axis, [(i, (i + step) % size) for i in range(size)])]
    dot_general x1 -> x2, matrix products: 12.8 us -> 18.9 us  [the longest x1 10.1 us: on_device(): jnp.dot(second, right_dense[block:], preferred_element_type=jnp.float32)]
    select_n x0 -> x2, other arithmetic: none -> 5.12 us  [the longest x1 3.48 us: on_device(): carried = jnp.where(col_index == panels[0], density, handed)]
    another operation x2 -> x0, other arithmetic: 4.73 us -> none  [on_device(): stacked = jnp.stack(lefts).reshape(2 * density.shape[0], density.shape[1])]
    pallas_call x3 -> x4, Pallas kernels: 34.1 us -> 37.5 us  [place(): pl.pallas_call(functools.partial(_place_kernel, src_blocks, dst_blocks, t...]
    ppermute x5 -> x7, starting transfers between devices: 8.31 us -> 8.28 us  [ring_shift(): return lax.ppermute(x, axis, [(i, (i + step) % size) for i in range(size)])]
  transfers between devices with their start and end apart: 7 -> 9, of which waited for: 6 -> 7; matrix products, arithmetic and copies ran while one was open for 3% -> 7% of each run, Pallas kernels for 3% -> 7%
where the time goes in v5:
time: 252 us; the launch traced here: 249 us
  waiting for transfers between devices  146 us (58%)
  Pallas kernels  37.5 us (15%)
  between operations  23.3 us (9%)
  matrix products  18.9 us (7%)
  other arithmetic  10.7 us (4%)
  starting transfers between devices  8.32 us (3%)
  local copies, waits for them, and re-layouts  4.3 us (2%)
    ppermute x7, waiting for transfers between devices, ring_shift(): return lax.ppermute(x, axis, [(i, (i + step) % size) for i in range(size)])  79.9 us
    all_gather x1, waiting for transfers between devices, on_device(): mine = lax.all_gather(part, ('cx', 'cz'), axis=0, tiled=True)  65.6 us
    pallas_call x4, Pallas kernels, place(): pl.pallas_call(functools.partial(_place_kernel, src_blocks, dst_blocks, t...  37.5 us
    dot_general x1, matrix products, on_device(): jnp.dot(second, right_dense[block:], preferred_element_type=jnp.float32)  10.1 us
    dot_general x1, matrix products, on_device(): jnp.dot(first, right_dense[:block], preferred_element_type=jnp.float32)  8.74 us
    ppermute x7, starting transfers between devices, ring_shift(): return lax.ppermute(x, axis, [(i, (i + step) % size) for i in range(size)])  8.28 us
  transfers between devices with their start and end apart: 9, of which 7 were waited for; matrix products, arithmetic and copies ran while one was open for 7% of the time, Pallas kernels for 7%

profile of v5, /device:TPU:32, one launch (start us, length us, event | category | flops | bytes accessed | tf_op | source)
XLA Modules:
  0.0 249.0 jit_solution(14492274331276592786)
XLA Ops:
  6.5 0.7 rev.3
  7.3 0.7 broadcast_compare_fusion
  8.0 0.7 fusion.9
  9.3 1.6 broadcast_select_fusion
  11.7 4.2 %collective-permute-done = bf16[3072,384]{1,0:T(8,128)(2,1)} collective-permute-done((bf16[3072,384]{1,0:T(8,128)(2,1)}, bf16[3072,384]{1,0:T(8,128)(2,1)}, u32[]{:S(2)}, u32[]{:S(2)}) %collective-permute-start) | collective-permute-done | bytes 2359328 | tf_op jit(solution)/shard_map/ppermute | solution.py:84
  15.9 3.5 %broadcast_select_fusion.1 = bf16[3072,384]{1,0:T(8,128)(2,1)} fusion(bf16[3072,384]{1,0:T(8,128)(2,1)S(1)} %copy-done, bf16[3072,384]{1,0:T(8,128)(2,1)} %collective-permute-done, pred[]{:T(512)S(6)} %eq.40), kind=kLoop, calls=%fused_computation.3 | loop fusion | flops 1179648 | bytes 7077889 | tf_op jit(solution)/shard_map/jit(_where)/select_n | solution.py:126
  25.0 0.2 select_bitcast_fusion.1
  25.2 0.1 pad_maximum_fusion
  25.4 1.9 collective-permute-start.1
  27.3 37.5 %collective-permute-done.1 = bf16[2,768,384]{2,1,0:T(8,128)(2,1)S(1)} collective-permute-done((bf16[2,768,384]{2,1,0:T(8,128)(2,1)S(1)}, bf16[2,768,384]{2,1,0:T(8,128)(2,1)S(1)}, u32[]{:S(2)}, u32[]{:S(2)}) %collective-permute-start.1) | collective-permute-done | bytes 1179680 | tf_op jit(solution)/shard_map/ppermute | solution.py:84
  64.8 0.2 broadcast_select_fusion.2
  65.0 3.1 %collective-permute-start.3 = (bf16[2,768,384]{2,1,0:T(8,128)(2,1)S(1)}, bf16[2,768,384]{2,1,0:T(8,128)(2,1)S(1)}, u32[]{:S(2)}, u32[]{:S(2)}) collective-permute-start(bf16[2,768,384]{2,1,0:T(8,128)(2,1)S(1)} %broadcast_select_fusion.2), channel_id=1, source_target_pairs={{0,96},{32,0},{64,32},{96,64},{1,97},{33,1},{65,33},{97,65},{2,98}... | collective-permute-start | bytes 3538952 | tf_op jit(solution)/shard_map/ppermute | solution.py:84
  68.1 24.1 %collective-permute-done.3 = bf16[2,768,384]{2,1,0:T(8,128)(2,1)S(1)} collective-permute-done((bf16[2,768,384]{2,1,0:T(8,128)(2,1)S(1)}, bf16[2,768,384]{2,1,0:T(8,128)(2,1)S(1)}, u32[]{:S(2)}, u32[]{:S(2)}) %collective-permute-start.3) | collective-permute-done | bytes 1179680 | tf_op jit(solution)/shard_map/ppermute | solution.py:84
  92.1 3.4 %collective-permute-done.2 = bf16[2,768,384]{2,1,0:T(8,128)(2,1)S(1)} collective-permute-done((bf16[2,768,384]{2,1,0:T(8,128)(2,1)S(1)}, bf16[2,768,384]{2,1,0:T(8,128)(2,1)S(1)}, u32[]{:S(2)}, u32[]{:S(2)}) %collective-permute-start.2) | collective-permute-done | bytes 1179680 | tf_op jit(solution)/shard_map/ppermute | solution.py:84
  95.6 0.4 select_select_fusion
  96.2 3.2 %collective-permute-start.5 = (bf16[2,384,384]{2,1,0:T(8,128)(2,1)S(1)}, bf16[2,384,384]{2,1,0:T(8,128)(2,1)S(1)}, u32[]{:S(2)}, u32[]{:S(2)}) collective-permute-start(bf16[2,384,384]{2,1,0:T(8,128)(2,1)S(1)} %get-tuple-element.16), channel_id=1, source_target_pairs={{0,96},{32,0},{64,32},{96,64},{1,97},{33,1},{65,33},{97,65},{2,98}... | collective-permute-start | bytes 1769480 | tf_op jit(solution)/shard_map/ppermute | solution.py:84
  99.4 10.7 %collective-permute-done.4 = bf16[2,384,384]{2,1,0:T(8,128)(2,1)S(1)} collective-permute-done((bf16[2,384,384]{2,1,0:T(8,128)(2,1)S(1)}, bf16[2,384,384]{2,1,0:T(8,128)(2,1)S(1)}, u32[]{:S(2)}, u32[]{:S(2)}) %collective-permute-start.4) | collective-permute-done | bytes 589856 | tf_op jit(solution)/shard_map/ppermute | solution.py:84
  110.2 1.5 maximum_select_fusion.values
  111.7 0.6 reduce-scatter.2.cloned.1.call-done
  112.2 65.6 %all-gather.2.cloned.1.call-done = bf16[3072,384]{1,0:T(8,128)(2,1)} async-done(((bf16[192,384]{1,0:T(8,128)(2,1)}), bf16[3072,384]{1,0:T(8,128)(2,1)}) %all-gather.2.cloned.1.call-update) | async-done | bytes 2359312 | tf_op jit(solution)/shard_map/all_gather | solution.py:134
  180.6 0.9 dynamic-slice_subtract_fusion.2
  181.9 0.9 dynamic-slice_subtract_fusion
  182.8 0.7 reshape.26.table
  183.6 0.7 reshape.23.table
  184.4 0.7 reshape.22.table
  185.2 0.6 pad_add_fusion.table
  185.8 6.3 %shard_map.38 = bf16[1536,768]{1,0:T(8,128)(2,1)} custom-call(s32[144]{0:T(256)} %pad_add_fusion.table, bf16[2,768,384]{2,1,0:T(8,128)(2,1)} %maximum_select_fusion.values), custom_call_target="tpu_custom_call" | custom-call | tf_op jit(solution)/shard_map/pallas_call | solution.py:71
  192.1 10.6 %shard_map.37 = bf16[3072,768]{1,0:T(8,128)(2,1)} custom-call(s32[288]{0:T(512)} %reshape.23.table, bf16[1,3072,384]{2,1,0:T(8,128)(2,1)} %bitcast.12), custom_call_target="tpu_custom_call" | custom-call | tf_op jit(solution)/shard_map/pallas_call | solution.py:71
  202.7 8.7 %fusion.2 = f32[3072,768]{1,0:T(8,128)} fusion(bf16[3072,768]{1,0:T(8,128)(2,1)} %shard_map.37, bf16[1536,768]{1,0:T(8,128)(2,1)S(1)} %copy-done.1), kind=kOutput, calls=%fused_computation.5 | convolution fusion | flops 3623878656 | bytes 15335424 | tf_op jit(solution)/shard_map/dot_general | solution.py:150
  211.5 10.5 %shard_map.39 = bf16[3072,768]{1,0:T(8,128)(2,1)} custom-call(s32[288]{0:T(512)} %reshape.26.table, bf16[1,3072,384]{2,1,0:T(8,128)(2,1)} %bitcast.5.values), custom_call_target="tpu_custom_call" | custom-call | tf_op jit(solution)/shard_map/pallas_call | solution.py:71
  222.0 10.1 %fusion.values = bf16[1,3072,768]{2,1,0:T(8,128)(2,1)} fusion(f32[3072,768]{1,0:T(8,128)} %fusion.2, bf16[3072,768]{1,0:T(8,128)(2,1)} %shard_map.39, bf16[1536,768]{1,0:T(8,128)(2,1)S(1)} %copy-done.1), kind=kOutput, calls=%fused_computation.1 | convolution fusion | flops 3628597248 | bytes 20054016 | tf_op jit(solution)/shard_map/dot_general | solution.py:151
  232.1 10.0 %shard_map.40 = bf16[3072,384]{1,0:T(8,128)(2,1)} custom-call(s32[288]{0:T(512)} %reshape.22.table, bf16[1,3072,768]{2,1,0:T(8,128)(2,1)} %fusion.values), custom_call_target="tpu_custom_call" | custom-call | tf_op jit(solution)/shard_map/pallas_call | solution.py:71
  (24 shorter events, 0.9 us)
Async XLA Ops:
  6.5 105.7 %reduce-scatter.2.cloned.1.call-start = ((), (), s32[]{:S(2)}) async-start(), calls=%async_computation.1 | async-start | bytes 2506752 | tf_op jit(solution)/shard_map/reduce_scatter | solution.py:127
  9.3 6.5 %copy-start = (bf16[3072,384]{1,0:T(8,128)(2,1)S(1)}, bf16[3072,384]{1,0:T(8,128)(2,1)}, u32[]{:S(2)}) copy-start(bf16[3072,384]{1,0:T(8,128)(2,1)} %param.3) | copy-start | bytes 7077892
  11.0 4.9 %collective-permute-start = (bf16[3072,384]{1,0:T(8,128)(2,1)}, bf16[3072,384]{1,0:T(8,128)(2,1)}, u32[]{:S(2)}, u32[]{:S(2)}) collective-permute-start(bf16[3072,384]{1,0:T(8,128)(2,1)} %broadcast_select_fusion), channel_id=1, source_target_pairs={{0,1},{1,0},{2,3},{3,2},{4,5},{5,4},{6,7},{7,6},{8,9},{9,8},{10,11... | collective-permute-start | bytes 7077896 | tf_op jit(solution)/shard_map/ppermute | solution.py:84
  19.4 158.4 %all-gather.2.cloned.1.call-start = ((), (), s32[]{:S(2)}) async-start(), calls=%async_computation.2 | async-start | bytes 2506752 | tf_op jit(solution)/shard_map/all_gather | solution.py:134
  25.4 39.4 %collective-permute-start.1 = (bf16[2,768,384]{2,1,0:T(8,128)(2,1)S(1)}, bf16[2,768,384]{2,1,0:T(8,128)(2,1)S(1)}, u32[]{:S(2)}, u32[]{:S(2)}) collective-permute-start(bf16[2,768,384]{2,1,0:T(8,128)(2,1)S(1)} %pad_maximum_fusion), channel_id=1, source_target_pairs={{0,128},{128,0},{1,129},{129,1},{2,130},{130,2},{3,131},{131,3},{4... | collective-permute-start | bytes 3538952 | tf_op jit(solution)/shard_map/ppermute | solution.py:84
  65.0 27.1 %collective-permute-start.3 = (bf16[2,768,384]{2,1,0:T(8,128)(2,1)S(1)}, bf16[2,768,384]{2,1,0:T(8,128)(2,1)S(1)}, u32[]{:S(2)}, u32[]{:S(2)}) collective-permute-start(bf16[2,768,384]{2,1,0:T(8,128)(2,1)S(1)} %broadcast_select_fusion.2), channel_id=1, source_target_pairs={{0,96},{32,0},{64,32},{96,64},{1,97},{33,1},{65,33},{97,65},{2,98}... | collective-permute-start | bytes 3538952 | tf_op jit(solution)/shard_map/ppermute | solution.py:84
  68.1 27.5 %collective-permute-start.2 = (bf16[2,768,384]{2,1,0:T(8,128)(2,1)S(1)}, bf16[2,768,384]{2,1,0:T(8,128)(2,1)S(1)}, u32[]{:S(2)}, u32[]{:S(2)}) collective-permute-start(bf16[2,768,384]{2,1,0:T(8,128)(2,1)S(1)} %broadcast_select_fusion.2), channel_id=1, source_target_pairs={{0,32},{32,64},{64,96},{96,0},{1,33},{33,65},{65,97},{97,1},{2,34}... | collective-permute-start | bytes 3538952 | tf_op jit(solution)/shard_map/ppermute | solution.py:84
  96.1 14.1 %collective-permute-start.4 = (bf16[2,384,384]{2,1,0:T(8,128)(2,1)S(1)}, bf16[2,384,384]{2,1,0:T(8,128)(2,1)S(1)}, u32[]{:S(2)}, u32[]{:S(2)}) collective-permute-start(bf16[2,384,384]{2,1,0:T(8,128)(2,1)S(1)} %get-tuple-element.15), channel_id=1, source_target_pairs={{0,32},{32,64},{64,96},{96,0},{1,33},{33,65},{65,97},{97,1},{2,34}... | collective-permute-start | bytes 1769480 | tf_op jit(solution)/shard_map/ppermute | solution.py:84
  96.2 14.0 %collective-permute-start.5 = (bf16[2,384,384]{2,1,0:T(8,128)(2,1)S(1)}, bf16[2,384,384]{2,1,0:T(8,128)(2,1)S(1)}, u32[]{:S(2)}, u32[]{:S(2)}) collective-permute-start(bf16[2,384,384]{2,1,0:T(8,128)(2,1)S(1)} %get-tuple-element.16), channel_id=1, source_target_pairs={{0,96},{32,0},{64,32},{96,64},{1,97},{33,1},{65,33},{97,65},{2,98}... | collective-permute-start | bytes 1769480 | tf_op jit(solution)/shard_map/ppermute | solution.py:84
  177.8 33.7 %collective-permute-start.6 = (bf16[3072,384]{1,0:T(8,128)(2,1)}, bf16[3072,384]{1,0:T(8,128)(2,1)}, u32[]{:S(2)}, u32[]{:S(2)}) collective-permute-start(bf16[3072,384]{1,0:T(8,128)(2,1)} %all-gather.2.cloned.1.call-done), channel_id=1, source_target_pairs={{0,1},{1,0},{2,3},{3,2},{4,5},{5,4},{6,7},{7,6},{8,9},{9,8},{10,11... | collective-permute-start | bytes 7077896 | tf_op jit(solution)/shard_map/ppermute | solution.py:84
  192.1 10.6 %copy-start.1 = (bf16[1536,768]{1,0:T(8,128)(2,1)S(1)}, bf16[1536,768]{1,0:T(8,128)(2,1)}, u32[]{:S(2)}) copy-start(bf16[1536,768]{1,0:T(8,128)(2,1)} %shard_map.38) | copy-start | bytes 7077892
Sparse Core Ops, SparseCore 0:
  19.5 92.6 reduce-scatter.1
  114.7 63.0 all-gather.1

commit v6 on v4

--- a/solution.py
+++ b/solution.py
@@ -23,7 +23,6 @@
     tile = pl.program_id(1)
     lanes = lax.broadcasted_iota(jnp.int32, (BLK, 2 * BLK), 1)
     high = lanes >= BLK
-    half = lanes // BLK
     placing = src_blocks < dst_blocks
     entries = src_blocks if placing else dst_blocks
     per_step = block_rows * entries
@@ -37,23 +36,25 @@
             a, b = _halves(values[0, rows, pl.ds(c * 2 * BLK, 2 * BLK)])
             plain.append(a)
             swapped.append(b)
-        sources = []
+        low = []
+        high_side = []
         for t in range(src_blocks):
             own = plain[t // 2]
             other = swapped[t // 2]
-            if t % 2 == 0:
-                sources.append(jnp.where(high, other, own))
-            else:
-                sources.append(jnp.where(high, own, other))
+            low.append(own if t % 2 == 0 else other)
+            high_side.append(other if t % 2 == 0 else own)
         for p in range(dst_blocks // 2):
-            acc = jnp.zeros((BLK, 2 * BLK), out.dtype)
+            acc_low = jnp.zeros((BLK, 2 * BLK), out.dtype)
+            acc_high = acc_low
             for t in range(src_blocks):
                 if placing:
-                    hit = half + 2 * p == table[base + t]
+                    entry = table[base + t]
+                    acc_low = jnp.where(entry == 2 * p, low[t], acc_low)
+                    acc_high = jnp.where(entry == 2 * p + 1, high_side[t], acc_high)
                 else:
-                    hit = jnp.where(high, table[base + 2 * p + 1], table[base + 2 * p]) == t
-                acc = jnp.where(hit, sources[t], acc)
-            out[rows, pl.ds(p * 2 * BLK, 2 * BLK)] = acc
+                    acc_low = jnp.where(table[base + 2 * p] == t, low[t], acc_low)
+                    acc_high = jnp.where(table[base + 2 * p + 1] == t, high_side[t], acc_high)
+            out[rows, pl.ds(p * 2 * BLK, 2 * BLK)] = jnp.where(high, acc_high, acc_low)
         return carry
 
     lax.fori_loop(0, tile_rows // BLK, one_row, 0)

time: 231 us -> 242 us (1.048)
  Pallas kernels: 34.1 us -> 47.3 us
    pallas_call x3, Pallas kernels: 34.1 us -> 47.3 us  [place(): pl.pallas_call(functools.partial(_place_kernel, src_blocks, dst_blocks, t...]
  transfers between devices with their start and end apart: 7 -> 7, of which waited for: 6 -> 6; matrix products, arithmetic and copies ran while one was open for 3% -> 3% of each run, Pallas kernels for 3% -> 4%
where the time goes in v6:
time: 242 us; the launch traced here: 240 us
  waiting for transfers between devices  135 us (56%)
  Pallas kernels  47.3 us (20%)
  between operations  23.1 us (10%)
  matrix products  12.8 us (5%)
  other arithmetic  10.3 us (4%)
  starting transfers between devices  8.36 us (3%)
  local copies, waits for them, and re-layouts  3.12 us (1%)
    ppermute x5, waiting for transfers between devices, ring_shift(): return lax.ppermute(x, axis, [(i, (i + step) % size) for i in range(size)])  65 us
    pallas_call x3, Pallas kernels, place(): pl.pallas_call(functools.partial(_place_kernel, src_blocks, dst_blocks, t...  47.3 us
    all_gather x1, waiting for transfers between devices, on_device(): lax.all_gather(part, COL_AXES, axis=0, tiled=True)  47.2 us
    reduce_scatter x1, waiting for transfers between devices, on_device(): part = lax.psum_scatter(stacked, COL_AXES, scatter_dimension=0, tiled=True)  22.6 us
    dot_general x1, matrix products, on_device(): jnp.dot(left_dense, right_dense, preferred_element_type=jnp.float32)  12.8 us
    ppermute x5, starting transfers between devices, ring_shift(): return lax.ppermute(x, axis, [(i, (i + step) % size) for i in range(size)])  8.31 us
  transfers between devices with their start and end apart: 7, of which 6 were waited for; matrix products, arithmetic and copies ran while one was open for 3% of the time, Pallas kernels for 4%

profile of v6, /device:TPU:32, one launch (start us, length us, event | category | flops | bytes accessed | tf_op | source)
XLA Modules:
  0.0 239.7 jit_solution(11390418226197237073)
XLA Ops:
  6.5 1.4 fusion.6
  9.3 2.1 select_bitcast_fusion.1
  11.4 2.6 %pad_maximum_fusion = bf16[2,3072,384]{2,1,0:T(8,128)(2,1)} fusion(bf16[1,3072,384]{2,1,0:T(8,128)(2,1)S(1)} %get-tuple-element.15, bf16[1,3072,384]{2,1,0:T(8,128)(2,1)S(1)} %get-tuple-element.14), kind=kLoop, calls=%fused_computation.1 | loop fusion | flops 2359296 | bytes 9437184 | tf_op jit(solution)/shard_map/stack | solution.py:126
  19.6 0.2 select_bitcast_fusion.3
  19.9 0.1 pad_maximum_fusion.1
  20.0 1.9 collective-permute-start
  22.0 25.8 %collective-permute-done = bf16[2,768,384]{2,1,0:T(8,128)(2,1)S(1)} collective-permute-done((bf16[2,768,384]{2,1,0:T(8,128)(2,1)S(1)}, bf16[2,768,384]{2,1,0:T(8,128)(2,1)S(1)}, u32[]{:S(2)}, u32[]{:S(2)}) %collective-permute-start) | collective-permute-done | bytes 1179680 | tf_op jit(solution)/shard_map/ppermute | solution.py:85
  47.8 0.2 broadcast_select_fusion
  48.1 1.7 collective-permute-start.1
  49.7 1.7 collective-permute-start.2
  51.4 24.9 %collective-permute-done.1 = bf16[2,768,384]{2,1,0:T(8,128)(2,1)S(1)} collective-permute-done((bf16[2,768,384]{2,1,0:T(8,128)(2,1)S(1)}, bf16[2,768,384]{2,1,0:T(8,128)(2,1)S(1)}, u32[]{:S(2)}, u32[]{:S(2)}) %collective-permute-start.1) | collective-permute-done | bytes 1179680 | tf_op jit(solution)/shard_map/ppermute | solution.py:85
  76.3 0.3 select_select_fusion
  76.6 0.1 fusion.5
  76.7 3.1 %collective-permute-start.4 = (bf16[2,384,384]{2,1,0:T(8,128)(2,1)S(1)}, bf16[2,384,384]{2,1,0:T(8,128)(2,1)S(1)}, u32[]{:S(2)}, u32[]{:S(2)}) collective-permute-start(bf16[2,384,384]{2,1,0:T(8,128)(2,1)S(1)} %get-tuple-element.17), channel_id=1, source_target_pairs={{0,96},{32,0},{64,32},{96,64},{1,97},{33,1},{65,33},{97,65},{2,98}... | collective-permute-start | bytes 1769480 | tf_op jit(solution)/shard_map/ppermute | solution.py:85
  79.8 10.8 %collective-permute-done.4 = bf16[2,384,384]{2,1,0:T(8,128)(2,1)S(1)} collective-permute-done((bf16[2,384,384]{2,1,0:T(8,128)(2,1)S(1)}, bf16[2,384,384]{2,1,0:T(8,128)(2,1)S(1)}, u32[]{:S(2)}, u32[]{:S(2)}) %collective-permute-start.4) | collective-permute-done | bytes 589856 | tf_op jit(solution)/shard_map/ppermute | solution.py:85
  90.7 3.4 %collective-permute-done.3 = bf16[2,384,384]{2,1,0:T(8,128)(2,1)S(1)} collective-permute-done((bf16[2,384,384]{2,1,0:T(8,128)(2,1)S(1)}, bf16[2,384,384]{2,1,0:T(8,128)(2,1)S(1)}, u32[]{:S(2)}, u32[]{:S(2)}) %collective-permute-start.3) | collective-permute-done | bytes 589856 | tf_op jit(solution)/shard_map/ppermute | solution.py:85
  94.1 1.5 maximum_select_fusion.values
  95.6 22.6 %reduce-scatter.2.cloned.1.call-done = bf16[192,384]{1,0:T(8,128)(2,1)} async-done(((bf16[6144,384]{1,0:T(8,128)(2,1)}), bf16[192,384]{1,0:T(8,128)(2,1)}) %reduce-scatter.2.cloned.1.call-update) | async-done | bytes 147472 | tf_op jit(solution)/shard_map/reduce_scatter | solution.py:127
  120.9 0.8 dynamic-slice_subtract_fusion.3
  121.9 0.7 reshape.28.table
  122.7 0.1 reshape.30
  122.9 0.1 reshape.29
  123.0 0.9 dynamic-slice_subtract_fusion.1
  123.9 0.1 copy.10
  124.1 0.1 copy.9
  124.3 0.7 pad_add_fusion.1.table
  125.0 0.6 pad_add_fusion.table
  125.6 8.4 %shard_map.38 = bf16[1536,768]{1,0:T(8,128)(2,1)} custom-call(s32[144]{0:T(256)} %pad_add_fusion.1.table, bf16[2,768,384]{2,1,0:T(8,128)(2,1)} %maximum_select_fusion.values), custom_call_target="tpu_custom_call" | custom-call | tf_op jit(solution)/shard_map/pallas_call | solution.py:72
  134.0 47.2 %all-gather.2.cloned.1.call-done = bf16[6144,384]{1,0:T(8,128)(2,1)} async-done(((bf16[192,384]{1,0:T(8,128)(2,1)}), bf16[6144,384]{1,0:T(8,128)(2,1)}) %all-gather.2.cloned.1.call-update) | async-done | bytes 4718608 | tf_op jit(solution)/shard_map/all_gather | solution.py:134
  181.2 26.5 %shard_map.37 = bf16[3072,1536]{1,0:T(8,128)(2,1)} custom-call(s32[576]{0:T(1024)} %pad_add_fusion.table, bf16[2,3072,384]{2,1,0:T(8,128)(2,1)} %bitcast.17), custom_call_target="tpu_custom_call" | custom-call | tf_op jit(solution)/shard_map/pallas_call | solution.py:72
  207.7 12.8 %fusion.values = bf16[1,3072,768]{2,1,0:T(8,128)(2,1)} fusion(bf16[3072,1536]{1,0:T(8,128)(2,1)} %shard_map.37, bf16[1536,768]{1,0:T(8,128)(2,1)S(1)} %copy-done.1), kind=kOutput, calls=%fused_computation.2 | convolution fusion | flops 7250116608 | bytes 16515072 | tf_op jit(solution)/shard_map/dot_general | solution.py:147
  220.4 12.4 %shard_map.39 = bf16[3072,384]{1,0:T(8,128)(2,1)} custom-call(s32[288]{0:T(512)} %reshape.28.table, bf16[1,3072,768]{2,1,0:T(8,128)(2,1)} %fusion.values), custom_call_target="tpu_custom_call" | custom-call | tf_op jit(solution)/shard_map/pallas_call | solution.py:72
  (20 shorter events, 0.6 us)
Async XLA Ops:
  6.5 111.7 %reduce-scatter.2.cloned.1.call-start = ((), (), s32[]{:S(2)}) async-start(), calls=%async_computation.1 | async-start | bytes 4866048 | tf_op jit(solution)/shard_map/reduce_scatter | solution.py:127
  14.0 5.6 %copy-start = (bf16[3072,384]{1,0:T(8,128)(2,1)S(1)}, bf16[3072,384]{1,0:T(8,128)(2,1)}, u32[]{:S(2)}) copy-start(bf16[3072,384]{1,0:T(8,128)(2,1)} %param.3) | copy-start | bytes 7077892
  14.0 167.2 %all-gather.2.cloned.1.call-start = ((), (), s32[]{:S(2)}) async-start(), calls=%async_computation.2 | async-start | bytes 4866048 | tf_op jit(solution)/shard_map/all_gather | solution.py:134
  19.9 2.1 copy-start.2
  20.0 27.8 %collective-permute-start = (bf16[2,768,384]{2,1,0:T(8,128)(2,1)S(1)}, bf16[2,768,384]{2,1,0:T(8,128)(2,1)S(1)}, u32[]{:S(2)}, u32[]{:S(2)}) collective-permute-start(bf16[2,768,384]{2,1,0:T(8,128)(2,1)S(1)} %pad_maximum_fusion.1), channel_id=1, source_target_pairs={{0,128},{128,0},{1,129},{129,1},{2,130},{130,2},{3,131},{131,3},{4... | collective-permute-start | bytes 3538952 | tf_op jit(solution)/shard_map/ppermute | solution.py:85
  48.1 28.2 %collective-permute-start.1 = (bf16[2,768,384]{2,1,0:T(8,128)(2,1)S(1)}, bf16[2,768,384]{2,1,0:T(8,128)(2,1)S(1)}, u32[]{:S(2)}, u32[]{:S(2)}) collective-permute-start(bf16[2,768,384]{2,1,0:T(8,128)(2,1)S(1)} %broadcast_select_fusion), channel_id=1, source_target_pairs={{0,32},{32,64},{64,96},{96,0},{1,33},{33,65},{65,97},{97,1},{2,34}... | collective-permute-start | bytes 3538952 | tf_op jit(solution)/shard_map/ppermute | solution.py:85
  49.7 26.6 %collective-permute-start.2 = (bf16[2,768,384]{2,1,0:T(8,128)(2,1)S(1)}, bf16[2,768,384]{2,1,0:T(8,128)(2,1)S(1)}, u32[]{:S(2)}, u32[]{:S(2)}) collective-permute-start(bf16[2,768,384]{2,1,0:T(8,128)(2,1)S(1)} %broadcast_select_fusion), channel_id=1, source_target_pairs={{0,96},{32,0},{64,32},{96,64},{1,97},{33,1},{65,33},{97,65},{2,98}... | collective-permute-start | bytes 3538952 | tf_op jit(solution)/shard_map/ppermute | solution.py:85
  76.7 13.9 %collective-permute-start.4 = (bf16[2,384,384]{2,1,0:T(8,128)(2,1)S(1)}, bf16[2,384,384]{2,1,0:T(8,128)(2,1)S(1)}, u32[]{:S(2)}, u32[]{:S(2)}) collective-permute-start(bf16[2,384,384]{2,1,0:T(8,128)(2,1)S(1)} %get-tuple-element.17), channel_id=1, source_target_pairs={{0,96},{32,0},{64,32},{96,64},{1,97},{33,1},{65,33},{97,65},{2,98}... | collective-permute-start | bytes 1769480 | tf_op jit(solution)/shard_map/ppermute | solution.py:85
  79.8 14.3 %collective-permute-start.3 = (bf16[2,384,384]{2,1,0:T(8,128)(2,1)S(1)}, bf16[2,384,384]{2,1,0:T(8,128)(2,1)S(1)}, u32[]{:S(2)}, u32[]{:S(2)}) collective-permute-start(bf16[2,384,384]{2,1,0:T(8,128)(2,1)S(1)} %get-tuple-element.16), channel_id=1, source_target_pairs={{0,32},{32,64},{64,96},{96,0},{1,33},{33,65},{65,97},{97,1},{2,34}... | collective-permute-start | bytes 1769480 | tf_op jit(solution)/shard_map/ppermute | solution.py:85
  181.2 26.5 %copy-start.1 = (bf16[1536,768]{1,0:T(8,128)(2,1)S(1)}, bf16[1536,768]{1,0:T(8,128)(2,1)}, u32[]{:S(2)}) copy-start(bf16[1536,768]{1,0:T(8,128)(2,1)} %shard_map.38) | copy-start | bytes 7077892
Sparse Core Ops, SparseCore 0:
  14.1 104.0 reduce-scatter.1
  120.7 60.3 all-gather.1

commit v7 on v4

--- a/solution.py
+++ b/solution.py
@@ -113,16 +113,17 @@
     my_rows = lax.dynamic_slice_in_dim(neighbours, row_index * row_blocks, row_blocks, 0)
     own_cols = lax.dynamic_slice_in_dim(my_rows, col_index * slot_count, slot_count, 1) - col_index * CB
 
+    own_dense = place(density[None], own_cols.reshape(-1), slot_count, CB, 1536, False)
     lefts = []
     bands = []
     for s in range(2):
         number = panels[s]
-        lefts.append(jnp.where(col_index == number, density, jnp.zeros_like(density)))
+        lefts.append(jnp.where(col_index == number, own_dense, jnp.zeros_like(own_dense)))
         offset = number % panels_per_row * CB * BLK
         band = lax.dynamic_slice_in_dim(density, offset, CB * BLK, 0)
         bands.append(jnp.where(row_index == number // panels_per_row, band, jnp.zeros_like(band)))
 
-    stacked = jnp.stack(lefts).reshape(2 * density.shape[0], density.shape[1])
+    stacked = jnp.stack(lefts).reshape(2 * own_dense.shape[0], own_dense.shape[1])
     part = lax.psum_scatter(stacked, COL_AXES, scatter_dimension=0, tiled=True)
 
     band_all = jnp.stack(bands)
@@ -130,20 +131,18 @@
     n_ry = lax.axis_size("ry")
     band_all = row_broadcast(band_all, owner_row // n_ry, owner_row % n_ry)
     part, band_all = lax.optimization_barrier((part, band_all))
-    left_all = lax.all_gather(part, COL_AXES, axis=0, tiled=True).reshape(2, *density.shape)
+    left_all = lax.all_gather(part, COL_AXES, axis=0, tiled=True).reshape(2, *own_dense.shape)
 
-    left_tables = []
     right_tables = []
     for s in range(2):
         number = panels[s]
-        group_cols = lax.dynamic_slice_in_dim(my_rows, number * slot_count, slot_count, 1) - number * CB
-        left_tables.append(group_cols.reshape(-1))
         band_rows = lax.dynamic_slice_in_dim(neighbours, number * CB, CB, 0)
         band_cols = lax.dynamic_slice_in_dim(band_rows, col_index * slot_count, slot_count, 1) - col_index * CB
         right_tables.append(band_cols.reshape(-1))
-    left_dense = place(left_all, jnp.concatenate(left_tables), slot_count, CB, 1536, False)
     right_dense = place(band_all, jnp.concatenate(right_tables), slot_count, CB, 768, True)
-    product = jnp.dot(left_dense, right_dense, preferred_element_type=jnp.float32).astype(jnp.bfloat16)
+    right_dense = right_dense.reshape(2, CB * BLK, CB * BLK)
+    product = jnp.einsum("sik,skj->ij", left_all, right_dense, preferred_element_type=jnp.float32)
+    product = product.astype(jnp.bfloat16)
     return place(product[None], own_cols.reshape(-1), CB, slot_count, 768, True)
 
 

time: 231 us -> 280 us (1.21)
  waiting for transfers between devices: 137 us -> 187 us
  other arithmetic: 10.2 us -> 19.8 us
  Pallas kernels: 34.1 us -> 26.8 us
    all_gather x1, waiting for transfers between devices: 49.3 us -> 75.5 us  [on_device(): lax.all_gather(part, COL_AXES, axis=0, tiled=True)]
    reduce_scatter x1, waiting for transfers between devices: 22.6 us -> 46.4 us  [on_device(): part = lax.psum_scatter(stacked, COL_AXES, scatter_dimension=0, tiled=True)]
    another operation x2, other arithmetic: 4.73 us -> 14.9 us  [on_device(): jnp.stack(lefts).reshape(2 * own_dense.shape[0], own_dense.shape[1])]
    pallas_call x3, Pallas kernels: 34.1 us -> 26.8 us  [place(): pl.pallas_call(functools.partial(_place_kernel, src_blocks, dst_blocks, t...]
  transfers between devices with their start and end apart: 7 -> 7, of which waited for: 6 -> 6; matrix products, arithmetic and copies ran while one was open for 3% -> 2% of each run, Pallas kernels for 3% -> 2%
where the time goes in v7:
time: 280 us; the launch traced here: 278 us
  waiting for transfers between devices  187 us (67%)
  Pallas kernels  26.8 us (10%)
  between operations  21.7 us (8%)
  other arithmetic  19.8 us (7%)
  matrix products  12.3 us (4%)
  starting transfers between devices  8.34 us (3%)
    all_gather x1, waiting for transfers between devices, on_device(): lax.all_gather(part, COL_AXES, axis=0, tiled=True)  75.5 us
    ppermute x5, waiting for transfers between devices, ring_shift(): return lax.ppermute(x, axis, [(i, (i + step) % size) for i in range(size)])  64.9 us
    reduce_scatter x1, waiting for transfers between devices, on_device(): part = lax.psum_scatter(stacked, COL_AXES, scatter_dimension=0, tiled=True)  46.4 us
    pallas_call x3, Pallas kernels, place(): pl.pallas_call(functools.partial(_place_kernel, src_blocks, dst_blocks, t...  26.8 us
    another operation x2, other arithmetic, on_device(): jnp.stack(lefts).reshape(2 * own_dense.shape[0], own_dense.shape[1])  14.9 us
    dot_general x1, matrix products, on_device(): jnp.einsum('sik,skj->ij', left_all, right_dense, preferred_element_type=j...  12.3 us
    ppermute x5, starting transfers between devices, ring_shift(): return lax.ppermute(x, axis, [(i, (i + step) % size) for i in range(size)])  8.29 us
  transfers between devices with their start and end apart: 7, of which 6 were waited for; matrix products, arithmetic and copies ran while one was open for 2% of the time, Pallas kernels for 2%

profile of v7, /device:TPU:32, one launch (start us, length us, event | category | flops | bytes accessed | tf_op | source)
XLA Modules:
  0.0 278.3 jit_solution(9872095718664766729)
XLA Ops:
  6.5 0.8 dynamic-slice_subtract_fusion.2
  7.3 0.1 copy.6
  7.4 0.7 reshape.26.table
  8.1 1.4 fusion.6
  10.9 10.4 %shard_map.37 = bf16[3072,768]{1,0:T(8,128)(2,1)} custom-call(s32[288]{0:T(512)} %reshape.26.table, bf16[1,3072,384]{2,1,0:T(8,128)(2,1)} %bitcast.23), custom_call_target="tpu_custom_call" | custom-call | tf_op jit(solution)/shard_map/pallas_call | solution.py:71
  21.3 6.7 %select_bitcast_fusion.1 = (bf16[1,3072,768]{2,1,0:T(8,128)(2,1)}, bf16[1,3072,768]{2,1,0:T(8,128)(2,1)}) fusion(bf16[3072,768]{1,0:T(8,128)(2,1)} %shard_map.37, pred[]{:T(512)S(6)} %eq.36, pred[]{:T(512)S(6)} %eq.37), kind=kLoop, calls=%fused_computation.3 | loop fusion | flops 4718592 | bytes 14155778 | tf_op jit(solution)/shard_map/stack | solution.py:126
  28.0 8.3 %pad_maximum_fusion = bf16[2,3072,768]{2,1,0:T(8,128)(2,1)} fusion(bf16[1,3072,768]{2,1,0:T(8,128)(2,1)} %get-tuple-element.13, bf16[1,3072,768]{2,1,0:T(8,128)(2,1)} %get-tuple-element.12), kind=kLoop, calls=%fused_computation | loop fusion | flops 4718592 | bytes 18874368 | tf_op jit(solution)/shard_map/stack | solution.py:126
  41.9 0.2 select_bitcast_fusion.3
  42.1 0.1 pad_maximum_fusion.1
  42.3 1.9 collective-permute-start
  44.2 25.8 %collective-permute-done = bf16[2,768,384]{2,1,0:T(8,128)(2,1)S(1)} collective-permute-done((bf16[2,768,384]{2,1,0:T(8,128)(2,1)S(1)}, bf16[2,768,384]{2,1,0:T(8,128)(2,1)S(1)}, u32[]{:S(2)}, u32[]{:S(2)}) %collective-permute-start) | collective-permute-done | bytes 1179680 | tf_op jit(solution)/shard_map/ppermute | solution.py:84
  70.1 0.2 broadcast_select_fusion
  70.3 1.7 collective-permute-start.1
  71.9 1.7 collective-permute-start.2
  73.6 24.9 %collective-permute-done.1 = bf16[2,768,384]{2,1,0:T(8,128)(2,1)S(1)} collective-permute-done((bf16[2,768,384]{2,1,0:T(8,128)(2,1)S(1)}, bf16[2,768,384]{2,1,0:T(8,128)(2,1)S(1)}, u32[]{:S(2)}, u32[]{:S(2)}) %collective-permute-start.1) | collective-permute-done | bytes 1179680 | tf_op jit(solution)/shard_map/ppermute | solution.py:84
  98.5 0.4 select_select_fusion
  98.9 0.1 fusion.5
  99.1 3.1 %collective-permute-start.4 = (bf16[2,384,384]{2,1,0:T(8,128)(2,1)S(1)}, bf16[2,384,384]{2,1,0:T(8,128)(2,1)S(1)}, u32[]{:S(2)}, u32[]{:S(2)}) collective-permute-start(bf16[2,384,384]{2,1,0:T(8,128)(2,1)S(1)} %get-tuple-element.17), channel_id=1, source_target_pairs={{0,96},{32,0},{64,32},{96,64},{1,97},{33,1},{65,33},{97,65},{2,98}... | collective-permute-start | bytes 1769480 | tf_op jit(solution)/shard_map/ppermute | solution.py:84
  102.1 10.7 %collective-permute-done.4 = bf16[2,384,384]{2,1,0:T(8,128)(2,1)S(1)} collective-permute-done((bf16[2,384,384]{2,1,0:T(8,128)(2,1)S(1)}, bf16[2,384,384]{2,1,0:T(8,128)(2,1)S(1)}, u32[]{:S(2)}, u32[]{:S(2)}) %collective-permute-start.4) | collective-permute-done | bytes 589856 | tf_op jit(solution)/shard_map/ppermute | solution.py:84
  112.9 3.4 %collective-permute-done.3 = bf16[2,384,384]{2,1,0:T(8,128)(2,1)S(1)} collective-permute-done((bf16[2,384,384]{2,1,0:T(8,128)(2,1)S(1)}, bf16[2,384,384]{2,1,0:T(8,128)(2,1)S(1)}, u32[]{:S(2)}, u32[]{:S(2)}) %collective-permute-start.3) | collective-permute-done | bytes 589856 | tf_op jit(solution)/shard_map/ppermute | solution.py:84
  116.3 1.5 maximum_select_fusion.values
  117.8 46.4 %reduce-scatter.2.cloned.1.call-done = bf16[192,768]{1,0:T(8,128)(2,1)} async-done(((bf16[6144,768]{1,0:T(8,128)(2,1)}), bf16[192,768]{1,0:T(8,128)(2,1)}) %reduce-scatter.2.cloned.1.call-update) | async-done | bytes 294928 | tf_op jit(solution)/shard_map/reduce_scatter | solution.py:127
  165.5 0.9 dynamic-slice_subtract_fusion.1
  166.4 0.1 copy.8
  166.5 0.1 reshape.30
  166.6 0.1 copy.7
  166.7 0.1 reshape.29
  166.8 0.6 pad_add_fusion.table
  167.4 6.3 %shard_map.38 = bf16[1536,768]{1,0:T(8,128)(2,1)} custom-call(s32[144]{0:T(256)} %pad_add_fusion.table, bf16[2,768,384]{2,1,0:T(8,128)(2,1)} %maximum_select_fusion.values), custom_call_target="tpu_custom_call" | custom-call | tf_op jit(solution)/shard_map/pallas_call | solution.py:71
  173.7 75.5 %all-gather.2.cloned.1.call-done = bf16[6144,768]{1,0:T(8,128)(2,1)} async-done(((bf16[192,768]{1,0:T(8,128)(2,1)}), bf16[6144,768]{1,0:T(8,128)(2,1)}) %all-gather.2.cloned.1.call-update) | async-done | bytes 9437200 | tf_op jit(solution)/shard_map/all_gather | solution.py:134
  249.2 12.3 %fusion.values = bf16[1,3072,768]{2,1,0:T(8,128)(2,1)} fusion(bf16[2,3072,768]{2,1,0:T(8,128)(2,1)} %bitcast.25, bf16[2,768,768]{2,1,0:T(8,128)(2,1)} %bitcast.24), kind=kOutput, calls=%fused_computation.4 | convolution fusion | flops 7250116608 | bytes 16515072 | tf_op jit(solution)/shard_map/sik,skj->ij/dot_general | solution.py:144
  261.4 10.0 %shard_map.39 = bf16[3072,384]{1,0:T(8,128)(2,1)} custom-call(s32[288]{0:T(512)} %reshape.26.table, bf16[1,3072,768]{2,1,0:T(8,128)(2,1)} %fusion.values), custom_call_target="tpu_custom_call" | custom-call | tf_op jit(solution)/shard_map/pallas_call | solution.py:71
  (13 shorter events, 0.2 us)
Async XLA Ops:
  6.5 157.6 %reduce-scatter.2.cloned.1.call-start = ((), (), s32[]{:S(2)}) async-start(), calls=%async_computation.1 | async-start | bytes 9732096 | tf_op jit(solution)/shard_map/reduce_scatter | solution.py:127
  36.3 5.6 %copy-start = (bf16[3072,384]{1,0:T(8,128)(2,1)S(1)}, bf16[3072,384]{1,0:T(8,128)(2,1)}, u32[]{:S(2)}) copy-start(bf16[3072,384]{1,0:T(8,128)(2,1)} %param.3) | copy-start | bytes 7077892
  36.3 212.9 %all-gather.2.cloned.1.call-start = ((), (), s32[]{:S(2)}) async-start(), calls=%async_computation.2 | async-start | bytes 9732096 | tf_op jit(solution)/shard_map/all_gather | solution.py:134
  41.9 2.3 copy-start.1
  42.3 27.8 %collective-permute-start = (bf16[2,768,384]{2,1,0:T(8,128)(2,1)S(1)}, bf16[2,768,384]{2,1,0:T(8,128)(2,1)S(1)}, u32[]{:S(2)}, u32[]{:S(2)}) collective-permute-start(bf16[2,768,384]{2,1,0:T(8,128)(2,1)S(1)} %pad_maximum_fusion.1), channel_id=1, source_target_pairs={{0,128},{128,0},{1,129},{129,1},{2,130},{130,2},{3,131},{131,3},{4... | collective-permute-start | bytes 3538952 | tf_op jit(solution)/shard_map/ppermute | solution.py:84
  70.3 28.2 %collective-permute-start.1 = (bf16[2,768,384]{2,1,0:T(8,128)(2,1)S(1)}, bf16[2,768,384]{2,1,0:T(8,128)(2,1)S(1)}, u32[]{:S(2)}, u32[]{:S(2)}) collective-permute-start(bf16[2,768,384]{2,1,0:T(8,128)(2,1)S(1)} %broadcast_select_fusion), channel_id=1, source_target_pairs={{0,32},{32,64},{64,96},{96,0},{1,33},{33,65},{65,97},{97,1},{2,34}... | collective-permute-start | bytes 3538952 | tf_op jit(solution)/shard_map/ppermute | solution.py:84
  71.9 26.6 %collective-permute-start.2 = (bf16[2,768,384]{2,1,0:T(8,128)(2,1)S(1)}, bf16[2,768,384]{2,1,0:T(8,128)(2,1)S(1)}, u32[]{:S(2)}, u32[]{:S(2)}) collective-permute-start(bf16[2,768,384]{2,1,0:T(8,128)(2,1)S(1)} %broadcast_select_fusion), channel_id=1, source_target_pairs={{0,96},{32,0},{64,32},{96,64},{1,97},{33,1},{65,33},{97,65},{2,98}... | collective-permute-start | bytes 3538952 | tf_op jit(solution)/shard_map/ppermute | solution.py:84
  99.1 13.8 %collective-permute-start.4 = (bf16[2,384,384]{2,1,0:T(8,128)(2,1)S(1)}, bf16[2,384,384]{2,1,0:T(8,128)(2,1)S(1)}, u32[]{:S(2)}, u32[]{:S(2)}) collective-permute-start(bf16[2,384,384]{2,1,0:T(8,128)(2,1)S(1)} %get-tuple-element.17), channel_id=1, source_target_pairs={{0,96},{32,0},{64,32},{96,64},{1,97},{33,1},{65,33},{97,65},{2,98}... | collective-permute-start | bytes 1769480 | tf_op jit(solution)/shard_map/ppermute | solution.py:84
  102.1 14.1 %collective-permute-start.3 = (bf16[2,384,384]{2,1,0:T(8,128)(2,1)S(1)}, bf16[2,384,384]{2,1,0:T(8,128)(2,1)S(1)}, u32[]{:S(2)}, u32[]{:S(2)}) collective-permute-start(bf16[2,384,384]{2,1,0:T(8,128)(2,1)S(1)} %get-tuple-element.16), channel_id=1, source_target_pairs={{0,32},{32,64},{64,96},{96,0},{1,33},{33,65},{65,97},{97,1},{2,34}... | collective-permute-start | bytes 1769480 | tf_op jit(solution)/shard_map/ppermute | solution.py:84
Sparse Core Ops, SparseCore 0:
  36.4 127.7 reduce-scatter.1
  166.7 82.4 all-gather.1

commit v8 on v4

--- a/solution.py
+++ b/solution.py
@@ -113,16 +113,16 @@
     my_rows = lax.dynamic_slice_in_dim(neighbours, row_index * row_blocks, row_blocks, 0)
     own_cols = lax.dynamic_slice_in_dim(my_rows, col_index * slot_count, slot_count, 1) - col_index * CB
 
-    lefts = []
+    roots = (col_index == panels)[:, None, None]
+    stacked = jnp.where(roots, density[None], jnp.zeros((), density.dtype))
     bands = []
     for s in range(2):
         number = panels[s]
-        lefts.append(jnp.where(col_index == number, density, jnp.zeros_like(density)))
         offset = number % panels_per_row * CB * BLK
         band = lax.dynamic_slice_in_dim(density, offset, CB * BLK, 0)
         bands.append(jnp.where(row_index == number // panels_per_row, band, jnp.zeros_like(band)))
 
-    stacked = jnp.stack(lefts).reshape(2 * density.shape[0], density.shape[1])
+    stacked = stacked.reshape(2 * density.shape[0], density.shape[1])
     part = lax.psum_scatter(stacked, COL_AXES, scatter_dimension=0, tiled=True)
 
     band_all = jnp.stack(bands)

time: 231 us -> 230 us (level)
    another operation x2 -> x0, other arithmetic: 4.73 us -> none  [on_device(): stacked = jnp.stack(lefts).reshape(2 * density.shape[0], density.shape[1])]
    select_n x0 -> x1, other arithmetic: none -> 4.71 us  [on_device(): stacked = jnp.where(roots, density[None], jnp.zeros((), density.dtype))]
where the time goes in v8:
time: 230 us; the launch traced here: 227 us
  waiting for transfers between devices  137 us (60%)
  Pallas kernels  34.1 us (15%)
  between operations  20.9 us (9%)
  matrix products  12.9 us (6%)
  other arithmetic  10.9 us (5%)
  starting transfers between devices  8.36 us (4%)
  local copies, waits for them, and re-layouts  2.97 us (1%)
    ppermute x5, waiting for transfers between devices, ring_shift(): return lax.ppermute(x, axis, [(i, (i + step) % size) for i in range(size)])  65 us
    all_gather x1, waiting for transfers between devices, on_device(): lax.all_gather(part, COL_AXES, axis=0, tiled=True)  49.5 us
    pallas_call x3, Pallas kernels, place(): pl.pallas_call(functools.partial(_place_kernel, src_blocks, dst_blocks, t...  34.1 us
    reduce_scatter x1, waiting for transfers between devices, on_device(): part = lax.psum_scatter(stacked, COL_AXES, scatter_dimension=0, tiled=True)  22.1 us
    dot_general x1, matrix products, on_device(): jnp.dot(left_dense, right_dense, preferred_element_type=jnp.float32)  12.9 us
    ppermute x5, starting transfers between devices, ring_shift(): return lax.ppermute(x, axis, [(i, (i + step) % size) for i in range(size)])  8.31 us
    select_n x1, other arithmetic, on_device(): stacked = jnp.where(roots, density[None], jnp.zeros((), density.dtype))  4.71 us
  transfers between devices with their start and end apart: 7, of which 6 were waited for; matrix products, arithmetic and copies ran while one was open for 3% of the time, Pallas kernels for 3%

profile of v8, /device:TPU:32, one launch (start us, length us, event | category | flops | bytes accessed | tf_op | source)
XLA Modules:
  0.0 226.8 jit_solution(13830609736427412262)
XLA Ops:
  6.5 0.7 broadcast_compare_fusion
  7.3 4.7 %bitcast_select_fusion = bf16[6144,384]{1,0:T(8,128)(2,1)} fusion(pred[6144]{0:T(1024)(128)(4,1)S(1)} %broadcast_in_dim.57, bf16[3072,384]{1,0:T(8,128)(2,1)} %param.3), kind=kLoop, calls=%fused_computation.1 | loop fusion | flops 2359296 | bytes 7084032 | tf_op jit(solution)/shard_map/jit(_where)/select_n | solution.py:117
  12.1 0.6 copy-done.2
  12.7 0.6 fusion.6
  18.2 0.2 select_bitcast_fusion.1
  18.4 0.1 pad_maximum_fusion
  18.6 1.9 collective-permute-start
  20.5 25.9 %collective-permute-done = bf16[2,768,384]{2,1,0:T(8,128)(2,1)S(1)} collective-permute-done((bf16[2,768,384]{2,1,0:T(8,128)(2,1)S(1)}, bf16[2,768,384]{2,1,0:T(8,128)(2,1)S(1)}, u32[]{:S(2)}, u32[]{:S(2)}) %collective-permute-start) | collective-permute-done | bytes 1179680 | tf_op jit(solution)/shard_map/ppermute | solution.py:84
  46.4 0.2 broadcast_select_fusion
  46.6 1.7 collective-permute-start.1
  48.3 1.7 collective-permute-start.2
  49.9 24.9 %collective-permute-done.1 = bf16[2,768,384]{2,1,0:T(8,128)(2,1)S(1)} collective-permute-done((bf16[2,768,384]{2,1,0:T(8,128)(2,1)S(1)}, bf16[2,768,384]{2,1,0:T(8,128)(2,1)S(1)}, u32[]{:S(2)}, u32[]{:S(2)}) %collective-permute-start.1) | collective-permute-done | bytes 1179680 | tf_op jit(solution)/shard_map/ppermute | solution.py:84
  74.8 0.3 select_select_fusion
  75.1 0.1 fusion.5
  75.3 3.1 %collective-permute-start.4 = (bf16[2,384,384]{2,1,0:T(8,128)(2,1)S(1)}, bf16[2,384,384]{2,1,0:T(8,128)(2,1)S(1)}, u32[]{:S(2)}, u32[]{:S(2)}) collective-permute-start(bf16[2,384,384]{2,1,0:T(8,128)(2,1)S(1)} %get-tuple-element.15), channel_id=1, source_target_pairs={{0,96},{32,0},{64,32},{96,64},{1,97},{33,1},{65,33},{97,65},{2,98}... | collective-permute-start | bytes 1769480 | tf_op jit(solution)/shard_map/ppermute | solution.py:84
  78.4 10.8 %collective-permute-done.4 = bf16[2,384,384]{2,1,0:T(8,128)(2,1)S(1)} collective-permute-done((bf16[2,384,384]{2,1,0:T(8,128)(2,1)S(1)}, bf16[2,384,384]{2,1,0:T(8,128)(2,1)S(1)}, u32[]{:S(2)}, u32[]{:S(2)}) %collective-permute-start.4) | collective-permute-done | bytes 589856 | tf_op jit(solution)/shard_map/ppermute | solution.py:84
  89.2 3.4 %collective-permute-done.3 = bf16[2,384,384]{2,1,0:T(8,128)(2,1)S(1)} collective-permute-done((bf16[2,384,384]{2,1,0:T(8,128)(2,1)S(1)}, bf16[2,384,384]{2,1,0:T(8,128)(2,1)S(1)}, u32[]{:S(2)}, u32[]{:S(2)}) %collective-permute-start.3) | collective-permute-done | bytes 589856 | tf_op jit(solution)/shard_map/ppermute | solution.py:84
  92.6 1.5 maximum_select_fusion.values
  94.2 22.1 %reduce-scatter.2.cloned.1.call-done = bf16[192,384]{1,0:T(8,128)(2,1)} async-done(((bf16[6144,384]{1,0:T(8,128)(2,1)}), bf16[192,384]{1,0:T(8,128)(2,1)}) %reduce-scatter.2.cloned.1.call-update) | async-done | bytes 147472 | tf_op jit(solution)/shard_map/reduce_scatter | solution.py:126
  118.7 0.8 dynamic-slice_subtract_fusion.3
  119.7 0.7 reshape.30.table
  120.5 0.1 reshape.32
  120.7 0.1 reshape.31
  120.8 0.9 dynamic-slice_subtract_fusion.1
  121.7 0.1 copy.10
  122.1 0.7 pad_add_fusion.1.table
  122.7 0.7 pad_add_fusion.table
  123.4 6.3 %shard_map.38 = bf16[1536,768]{1,0:T(8,128)(2,1)} custom-call(s32[144]{0:T(256)} %pad_add_fusion.1.table, bf16[2,768,384]{2,1,0:T(8,128)(2,1)} %maximum_select_fusion.values), custom_call_target="tpu_custom_call" | custom-call | tf_op jit(solution)/shard_map/pallas_call | solution.py:71
  129.7 49.5 %all-gather.2.cloned.1.call-done = bf16[6144,384]{1,0:T(8,128)(2,1)} async-done(((bf16[192,384]{1,0:T(8,128)(2,1)}), bf16[6144,384]{1,0:T(8,128)(2,1)}) %all-gather.2.cloned.1.call-update) | async-done | bytes 4718608 | tf_op jit(solution)/shard_map/all_gather | solution.py:133
  179.2 17.8 %shard_map.37 = bf16[3072,1536]{1,0:T(8,128)(2,1)} custom-call(s32[576]{0:T(1024)} %pad_add_fusion.table, bf16[2,3072,384]{2,1,0:T(8,128)(2,1)} %bitcast.13), custom_call_target="tpu_custom_call" | custom-call | tf_op jit(solution)/shard_map/pallas_call | solution.py:71
  197.0 12.9 %fusion.values = bf16[1,3072,768]{2,1,0:T(8,128)(2,1)} fusion(bf16[3072,1536]{1,0:T(8,128)(2,1)} %shard_map.37, bf16[1536,768]{1,0:T(8,128)(2,1)S(1)} %copy-done.1), kind=kOutput, calls=%fused_computation.2 | convolution fusion | flops 7250116608 | bytes 16515072 | tf_op jit(solution)/shard_map/dot_general | solution.py:146
  209.9 10.0 %shard_map.39 = bf16[3072,384]{1,0:T(8,128)(2,1)} custom-call(s32[288]{0:T(512)} %reshape.30.table, bf16[1,3072,768]{2,1,0:T(8,128)(2,1)} %fusion.values), custom_call_target="tpu_custom_call" | custom-call | tf_op jit(solution)/shard_map/pallas_call | solution.py:71
  (21 shorter events, 0.8 us)
Async XLA Ops:
  6.5 109.7 %reduce-scatter.2.cloned.1.call-start = ((), (), s32[]{:S(2)}) async-start(), calls=%async_computation.1 | async-start | bytes 4866048 | tf_op jit(solution)/shard_map/reduce_scatter | solution.py:126
  12.0 0.7 copy-start.2
  12.0 6.1 %copy-start = (bf16[3072,384]{1,0:T(8,128)(2,1)S(1)}, bf16[3072,384]{1,0:T(8,128)(2,1)}, u32[]{:S(2)}) copy-start(bf16[3072,384]{1,0:T(8,128)(2,1)} %param.3) | copy-start | bytes 7077892
  12.1 167.2 %all-gather.2.cloned.1.call-start = ((), (), s32[]{:S(2)}) async-start(), calls=%async_computation.2 | async-start | bytes 4866048 | tf_op jit(solution)/shard_map/all_gather | solution.py:133
  18.6 27.8 %collective-permute-start = (bf16[2,768,384]{2,1,0:T(8,128)(2,1)S(1)}, bf16[2,768,384]{2,1,0:T(8,128)(2,1)S(1)}, u32[]{:S(2)}, u32[]{:S(2)}) collective-permute-start(bf16[2,768,384]{2,1,0:T(8,128)(2,1)S(1)} %pad_maximum_fusion), channel_id=1, source_target_pairs={{0,128},{128,0},{1,129},{129,1},{2,130},{130,2},{3,131},{131,3},{4... | collective-permute-start | bytes 3538952 | tf_op jit(solution)/shard_map/ppermute | solution.py:84
  46.6 28.2 %collective-permute-start.1 = (bf16[2,768,384]{2,1,0:T(8,128)(2,1)S(1)}, bf16[2,768,384]{2,1,0:T(8,128)(2,1)S(1)}, u32[]{:S(2)}, u32[]{:S(2)}) collective-permute-start(bf16[2,768,384]{2,1,0:T(8,128)(2,1)S(1)} %broadcast_select_fusion), channel_id=1, source_target_pairs={{0,32},{32,64},{64,96},{96,0},{1,33},{33,65},{65,97},{97,1},{2,34}... | collective-permute-start | bytes 3538952 | tf_op jit(solution)/shard_map/ppermute | solution.py:84
  48.3 26.6 %collective-permute-start.2 = (bf16[2,768,384]{2,1,0:T(8,128)(2,1)S(1)}, bf16[2,768,384]{2,1,0:T(8,128)(2,1)S(1)}, u32[]{:S(2)}, u32[]{:S(2)}) collective-permute-start(bf16[2,768,384]{2,1,0:T(8,128)(2,1)S(1)} %broadcast_select_fusion), channel_id=1, source_target_pairs={{0,96},{32,0},{64,32},{96,64},{1,97},{33,1},{65,33},{97,65},{2,98}... | collective-permute-start | bytes 3538952 | tf_op jit(solution)/shard_map/ppermute | solution.py:84
  75.3 13.9 %collective-permute-start.4 = (bf16[2,384,384]{2,1,0:T(8,128)(2,1)S(1)}, bf16[2,384,384]{2,1,0:T(8,128)(2,1)S(1)}, u32[]{:S(2)}, u32[]{:S(2)}) collective-permute-start(bf16[2,384,384]{2,1,0:T(8,128)(2,1)S(1)} %get-tuple-element.15), channel_id=1, source_target_pairs={{0,96},{32,0},{64,32},{96,64},{1,97},{33,1},{65,33},{97,65},{2,98}... | collective-permute-start | bytes 1769480 | tf_op jit(solution)/shard_map/ppermute | solution.py:84
  78.4 14.3 %collective-permute-start.3 = (bf16[2,384,384]{2,1,0:T(8,128)(2,1)S(1)}, bf16[2,384,384]{2,1,0:T(8,128)(2,1)S(1)}, u32[]{:S(2)}, u32[]{:S(2)}) collective-permute-start(bf16[2,384,384]{2,1,0:T(8,128)(2,1)S(1)} %get-tuple-element.14), channel_id=1, source_target_pairs={{0,32},{32,64},{64,96},{96,0},{1,33},{33,65},{65,97},{97,1},{2,34}... | collective-permute-start | bytes 1769480 | tf_op jit(solution)/shard_map/ppermute | solution.py:84
  179.2 17.8 %copy-start.1 = (bf16[1536,768]{1,0:T(8,128)(2,1)S(1)}, bf16[1536,768]{1,0:T(8,128)(2,1)}, u32[]{:S(2)}) copy-start(bf16[1536,768]{1,0:T(8,128)(2,1)} %shard_map.38) | copy-start | bytes 7077892
Sparse Core Ops, SparseCore 0:
  12.2 104.0 reduce-scatter.1
  118.8 60.4 all-gather.1

commit v9 on v8

--- a/solution.py
+++ b/solution.py
@@ -57,6 +57,31 @@
         return carry
 
     lax.fori_loop(0, tile_rows // BLK, one_row, 0)
+
+
+def _product_pick_kernel(tile_rows, block_rows, table, left, right, out, product):
+    product[0] = jnp.dot(left[...], right[...], preferred_element_type=jnp.float32).astype(product.dtype)
+    _place_kernel(CB, out.shape[1] // BLK, tile_rows, block_rows, table, product, out)
+
+
+def product_pick(left, right, table, tile_rows):
+    rows = left.shape[0]
+    width = right.shape[1]
+    slots = table.shape[0] // (rows // BLK)
+    return pl.pallas_call(
+        functools.partial(_product_pick_kernel, tile_rows, rows // BLK),
+        out_shape=jax.ShapeDtypeStruct((rows, slots * BLK), left.dtype),
+        grid_spec=pltpu.PrefetchScalarGridSpec(
+            num_scalar_prefetch=1,
+            grid=(1, rows // tile_rows),
+            in_specs=[
+                pl.BlockSpec((tile_rows, left.shape[1]), lambda s, g, tab: (g, 0)),
+                pl.BlockSpec(right.shape, lambda s, g, tab: (0, 0)),
+            ],
+            out_specs=pl.BlockSpec((tile_rows, slots * BLK), lambda s, g, tab: (g, 0)),
+            scratch_shapes=[pltpu.VMEM((1, tile_rows, width), left.dtype)],
+        ),
+    )(table, left, right)
 
 
 def place(values, table, src_blocks, dst_blocks, tile_rows, by_rows):
@@ -143,8 +168,7 @@
         right_tables.append(band_cols.reshape(-1))
     left_dense = place(left_all, jnp.concatenate(left_tables), slot_count, CB, 1536, False)
     right_dense = place(band_all, jnp.concatenate(right_tables), slot_count, CB, 768, True)
-    product = jnp.dot(left_dense, right_dense, preferred_element_type=jnp.float32).astype(jnp.bfloat16)
-    return place(product[None], own_cols.reshape(-1), CB, slot_count, 768, True)
+    return product_pick(left_dense, right_dense, own_cols.reshape(-1), 256)
 
 
 def solution(mesh):

time: 230 us -> 227 us (0.987)
  matrix products: 12.9 us -> 0 us
  Pallas kernels: 34.1 us -> 44.1 us
    pallas_call x0 -> x1, Pallas kernels: none -> 20.1 us  [product_pick(): pl.pallas_call(functools.partial(_product_pick_kernel, tile_rows, rows //...]
    dot_general x1 -> x0, matrix products: 12.9 us -> none  [on_device(): jnp.dot(left_dense, right_dense, preferred_element_type=jnp.float32)]
    pallas_call x3 -> x2, Pallas kernels: 34.1 us -> 24 us  [place(): pl.pallas_call(functools.partial(_place_kernel, src_blocks, dst_blocks, t...]
where the time goes in v9:
time: 227 us; the launch traced here: 224 us
  waiting for transfers between devices  137 us (60%)
  Pallas kernels  44.1 us (19%)
  between operations  21 us (9%)
  other arithmetic  10.8 us (5%)
  starting transfers between devices  8.36 us (4%)
  local copies, waits for them, and re-layouts  2.99 us (1%)
    ppermute x5, waiting for transfers between devices, ring_shift(): return lax.ppermute(x, axis, [(i, (i + step) % size) for i in range(size)])  65 us
    all_gather x1, waiting for transfers between devices, on_device(): lax.all_gather(part, COL_AXES, axis=0, tiled=True)  49.5 us
    pallas_call x2, Pallas kernels, place(): pl.pallas_call(functools.partial(_place_kernel, src_blocks, dst_blocks, t...  24 us
    reduce_scatter x1, waiting for transfers between devices, on_device(): part = lax.psum_scatter(stacked, COL_AXES, scatter_dimension=0, tiled=True)  22 us
    pallas_call x1, Pallas kernels, product_pick(): pl.pallas_call(functools.partial(_product_pick_kernel, tile_rows, rows //...  20.1 us
    ppermute x5, starting transfers between devices, ring_shift(): return lax.ppermute(x, axis, [(i, (i + step) % size) for i in range(size)])  8.31 us
    select_n x1, other arithmetic, on_device(): stacked = jnp.where(roots, density[None], jnp.zeros((), density.dtype))  4.71 us
  transfers between devices with their start and end apart: 7, of which 6 were waited for; matrix products, arithmetic and copies ran while one was open for 3% of the time, Pallas kernels for 3%

profile of v9, /device:TPU:32, one launch (start us, length us, event | category | flops | bytes accessed | tf_op | source)
XLA Modules:
  0.0 223.8 jit_solution(17382993817722936392)
XLA Ops:
  6.5 0.7 broadcast_compare_fusion
  7.3 4.7 %bitcast_select_fusion = bf16[6144,384]{1,0:T(8,128)(2,1)} fusion(pred[6144]{0:T(1024)(128)(4,1)S(1)} %broadcast_in_dim.54, bf16[3072,384]{1,0:T(8,128)(2,1)} %param.3), kind=kLoop, calls=%fused_computation | loop fusion | flops 2359296 | bytes 7084032 | tf_op jit(solution)/shard_map/jit(_where)/select_n | solution.py:142
  12.1 0.6 copy-done.1
  12.7 0.6 fusion.5
  18.4 0.2 select_bitcast_fusion.1
  18.6 0.1 pad_maximum_fusion
  18.7 1.9 collective-permute-start
  20.6 25.9 %collective-permute-done = bf16[2,768,384]{2,1,0:T(8,128)(2,1)S(1)} collective-permute-done((bf16[2,768,384]{2,1,0:T(8,128)(2,1)S(1)}, bf16[2,768,384]{2,1,0:T(8,128)(2,1)S(1)}, u32[]{:S(2)}, u32[]{:S(2)}) %collective-permute-start) | collective-permute-done | bytes 1179680 | tf_op jit(solution)/shard_map/ppermute | solution.py:109
  46.5 0.2 broadcast_select_fusion
  46.7 1.7 collective-permute-start.1
  48.4 1.7 collective-permute-start.2
  50.1 24.9 %collective-permute-done.1 = bf16[2,768,384]{2,1,0:T(8,128)(2,1)S(1)} collective-permute-done((bf16[2,768,384]{2,1,0:T(8,128)(2,1)S(1)}, bf16[2,768,384]{2,1,0:T(8,128)(2,1)S(1)}, u32[]{:S(2)}, u32[]{:S(2)}) %collective-permute-start.1) | collective-permute-done | bytes 1179680 | tf_op jit(solution)/shard_map/ppermute | solution.py:109
  75.0 0.3 select_select_fusion
  75.3 0.1 fusion.4
  75.4 3.1 %collective-permute-start.4 = (bf16[2,384,384]{2,1,0:T(8,128)(2,1)S(1)}, bf16[2,384,384]{2,1,0:T(8,128)(2,1)S(1)}, u32[]{:S(2)}, u32[]{:S(2)}) collective-permute-start(bf16[2,384,384]{2,1,0:T(8,128)(2,1)S(1)} %get-tuple-element.15), channel_id=1, source_target_pairs={{0,96},{32,0},{64,32},{96,64},{1,97},{33,1},{65,33},{97,65},{2,98}... | collective-permute-start | bytes 1769480 | tf_op jit(solution)/shard_map/ppermute | solution.py:109
  78.5 10.8 %collective-permute-done.4 = bf16[2,384,384]{2,1,0:T(8,128)(2,1)S(1)} collective-permute-done((bf16[2,384,384]{2,1,0:T(8,128)(2,1)S(1)}, bf16[2,384,384]{2,1,0:T(8,128)(2,1)S(1)}, u32[]{:S(2)}, u32[]{:S(2)}) %collective-permute-start.4) | collective-permute-done | bytes 589856 | tf_op jit(solution)/shard_map/ppermute | solution.py:109
  89.4 3.4 %collective-permute-done.3 = bf16[2,384,384]{2,1,0:T(8,128)(2,1)S(1)} collective-permute-done((bf16[2,384,384]{2,1,0:T(8,128)(2,1)S(1)}, bf16[2,384,384]{2,1,0:T(8,128)(2,1)S(1)}, u32[]{:S(2)}, u32[]{:S(2)}) %collective-permute-start.3) | collective-permute-done | bytes 589856 | tf_op jit(solution)/shard_map/ppermute | solution.py:109
  92.8 1.5 maximum_select_fusion.values
  94.3 22.0 %reduce-scatter.2.cloned.1.call-done = bf16[192,384]{1,0:T(8,128)(2,1)} async-done(((bf16[6144,384]{1,0:T(8,128)(2,1)}), bf16[192,384]{1,0:T(8,128)(2,1)}) %reduce-scatter.2.cloned.1.call-update) | async-done | bytes 147472 | tf_op jit(solution)/shard_map/reduce_scatter | solution.py:151
  118.8 0.8 dynamic-slice_subtract_fusion.3
  119.7 0.7 reshape.30.table
  120.5 0.1 reshape.32
  120.7 0.1 reshape.31
  120.9 0.9 dynamic-slice_subtract_fusion.1
  121.7 0.1 copy.10
  121.9 0.1 copy.9
  122.1 0.6 pad_add_fusion.1.table
  122.7 0.7 pad_add_fusion.table
  123.4 6.3 %shard_map.38.right = bf16[1536,768]{1,0:T(8,128)(2,1)} custom-call(s32[144]{0:T(256)} %pad_add_fusion.1.table, bf16[2,768,384]{2,1,0:T(8,128)(2,1)} %maximum_select_fusion.values), custom_call_target="tpu_custom_call" | custom-call | tf_op jit(solution)/shard_map/pallas_call | solution.py:96
  129.7 49.5 %all-gather.2.cloned.1.call-done = bf16[6144,384]{1,0:T(8,128)(2,1)} async-done(((bf16[192,384]{1,0:T(8,128)(2,1)}), bf16[6144,384]{1,0:T(8,128)(2,1)}) %all-gather.2.cloned.1.call-update) | async-done | bytes 4718608 | tf_op jit(solution)/shard_map/all_gather | solution.py:158
  179.2 17.7 %shard_map.37.left = bf16[3072,1536]{1,0:T(8,128)(2,1)} custom-call(s32[576]{0:T(1024)} %pad_add_fusion.table, bf16[2,3072,384]{2,1,0:T(8,128)(2,1)} %bitcast.9), custom_call_target="tpu_custom_call" | custom-call | tf_op jit(solution)/shard_map/pallas_call | solution.py:96
  196.9 20.1 %shard_map.39 = bf16[3072,384]{1,0:T(8,128)(2,1)} custom-call(s32[288]{0:T(512)} %reshape.30.table, bf16[3072,1536]{1,0:T(8,128)(2,1)} %shard_map.37.left, bf16[1536,768]{1,0:T(8,128)(2,1)} %shard_map.38.right), custom_call_target="tpu_custom_call" | custom-call | tf_op jit(solution)/shard_map/pallas_call | solution.py:71
  (18 shorter events, 0.7 us)
Async XLA Ops:
  6.5 109.7 %reduce-scatter.2.cloned.1.call-start = ((), (), s32[]{:S(2)}) async-start(), calls=%async_computation.1 | async-start | bytes 4866048 | tf_op jit(solution)/shard_map/reduce_scatter | solution.py:151
  12.0 0.7 copy-start.1
  12.0 6.3 %copy-start = (bf16[3072,384]{1,0:T(8,128)(2,1)S(1)}, bf16[3072,384]{1,0:T(8,128)(2,1)}, u32[]{:S(2)}) copy-start(bf16[3072,384]{1,0:T(8,128)(2,1)} %param.3) | copy-start | bytes 7077892
  12.1 167.2 %all-gather.2.cloned.1.call-start = ((), (), s32[]{:S(2)}) async-start(), calls=%async_computation.2 | async-start | bytes 4866048 | tf_op jit(solution)/shard_map/all_gather | solution.py:158
  18.7 27.8 %collective-permute-start = (bf16[2,768,384]{2,1,0:T(8,128)(2,1)S(1)}, bf16[2,768,384]{2,1,0:T(8,128)(2,1)S(1)}, u32[]{:S(2)}, u32[]{:S(2)}) collective-permute-start(bf16[2,768,384]{2,1,0:T(8,128)(2,1)S(1)} %pad_maximum_fusion), channel_id=1, source_target_pairs={{0,128},{128,0},{1,129},{129,1},{2,130},{130,2},{3,131},{131,3},{4... | collective-permute-start | bytes 3538952 | tf_op jit(solution)/shard_map/ppermute | solution.py:109
  46.7 28.2 %collective-permute-start.1 = (bf16[2,768,384]{2,1,0:T(8,128)(2,1)S(1)}, bf16[2,768,384]{2,1,0:T(8,128)(2,1)S(1)}, u32[]{:S(2)}, u32[]{:S(2)}) collective-permute-start(bf16[2,768,384]{2,1,0:T(8,128)(2,1)S(1)} %broadcast_select_fusion), channel_id=1, source_target_pairs={{0,32},{32,64},{64,96},{96,0},{1,33},{33,65},{65,97},{97,1},{2,34}... | collective-permute-start | bytes 3538952 | tf_op jit(solution)/shard_map/ppermute | solution.py:109
  48.4 26.6 %collective-permute-start.2 = (bf16[2,768,384]{2,1,0:T(8,128)(2,1)S(1)}, bf16[2,768,384]{2,1,0:T(8,128)(2,1)S(1)}, u32[]{:S(2)}, u32[]{:S(2)}) collective-permute-start(bf16[2,768,384]{2,1,0:T(8,128)(2,1)S(1)} %broadcast_select_fusion), channel_id=1, source_target_pairs={{0,96},{32,0},{64,32},{96,64},{1,97},{33,1},{65,33},{97,65},{2,98}... | collective-permute-start | bytes 3538952 | tf_op jit(solution)/shard_map/ppermute | solution.py:109
  75.4 13.9 %collective-permute-start.4 = (bf16[2,384,384]{2,1,0:T(8,128)(2,1)S(1)}, bf16[2,384,384]{2,1,0:T(8,128)(2,1)S(1)}, u32[]{:S(2)}, u32[]{:S(2)}) collective-permute-start(bf16[2,384,384]{2,1,0:T(8,128)(2,1)S(1)} %get-tuple-element.15), channel_id=1, source_target_pairs={{0,96},{32,0},{64,32},{96,64},{1,97},{33,1},{65,33},{97,65},{2,98}... | collective-permute-start | bytes 1769480 | tf_op jit(solution)/shard_map/ppermute | solution.py:109
  78.5 14.3 %collective-permute-start.3 = (bf16[2,384,384]{2,1,0:T(8,128)(2,1)S(1)}, bf16[2,384,384]{2,1,0:T(8,128)(2,1)S(1)}, u32[]{:S(2)}, u32[]{:S(2)}) collective-permute-start(bf16[2,384,384]{2,1,0:T(8,128)(2,1)S(1)} %get-tuple-element.14), channel_id=1, source_target_pairs={{0,32},{32,64},{64,96},{96,0},{1,33},{33,65},{65,97},{97,1},{2,34}... | collective-permute-start | bytes 1769480 | tf_op jit(solution)/shard_map/ppermute | solution.py:109
Sparse Core Ops, SparseCore 0:
  12.2 104.0 reduce-scatter.1
  118.8 60.4 all-gather.1

commit v10 on v9

--- a/solution.py
+++ b/solution.py
@@ -19,8 +19,10 @@
 
 
 def _place_kernel(src_blocks, dst_blocks, tile_rows, block_rows, table, values, out):
-    step = pl.program_id(0)
-    tile = pl.program_id(1)
+    _place_body(src_blocks, dst_blocks, tile_rows, block_rows, table, values, out, pl.program_id(0), pl.program_id(1), 0)
+
+
+def _place_body(src_blocks, dst_blocks, tile_rows, block_rows, table, values, out, step, tile, offset):
     lanes = lax.broadcasted_iota(jnp.int32, (BLK, 2 * BLK), 1)
     high = lanes >= BLK
     half = lanes // BLK
@@ -29,7 +31,7 @@
     per_step = block_rows * entries
 
     def one_row(q, carry):
-        base = step * per_step + (tile * (tile_rows // BLK) + q) * entries
+        base = offset + step * per_step + (tile * (tile_rows // BLK) + q) * entries
         rows = pl.ds(pl.multiple_of(q * BLK, BLK), BLK)
         plain = []
         swapped = []
@@ -59,27 +61,34 @@
     lax.fori_loop(0, tile_rows // BLK, one_row, 0)
 
 
-def _product_pick_kernel(tile_rows, block_rows, table, left, right, out, product):
-    product[0] = jnp.dot(left[...], right[...], preferred_element_type=jnp.float32).astype(product.dtype)
-    _place_kernel(CB, out.shape[1] // BLK, tile_rows, block_rows, table, product, out)
+def _fused_kernel(tile_rows, block_rows, slots, table, left, right, out, dense, product):
+    tile = pl.program_id(1)
+    steps = left.shape[0]
+    width = CB * BLK
+    for s in range(steps):
+        view = dense.at[:, pl.ds(s * width, width)]
+        _place_body(slots, CB, tile_rows, block_rows, table, left.at[pl.ds(s, 1)], view, s, tile, 0)
+    product[0] = jnp.dot(dense[...], right[...], preferred_element_type=jnp.float32).astype(product.dtype)
+    _place_body(CB, slots, tile_rows, block_rows, table, product, out, 0, tile, steps * block_rows * slots)
 
 
-def product_pick(left, right, table, tile_rows):
-    rows = left.shape[0]
-    width = right.shape[1]
-    slots = table.shape[0] // (rows // BLK)
+def fused_product(left, right, table, slots, tile_rows):
+    steps, rows, _ = left.shape
     return pl.pallas_call(
-        functools.partial(_product_pick_kernel, tile_rows, rows // BLK),
+        functools.partial(_fused_kernel, tile_rows, rows // BLK, slots),
         out_shape=jax.ShapeDtypeStruct((rows, slots * BLK), left.dtype),
         grid_spec=pltpu.PrefetchScalarGridSpec(
             num_scalar_prefetch=1,
             grid=(1, rows // tile_rows),
             in_specs=[
-                pl.BlockSpec((tile_rows, left.shape[1]), lambda s, g, tab: (g, 0)),
+                pl.BlockSpec((steps, tile_rows, left.shape[2]), lambda s, g, tab: (0, g, 0)),
                 pl.BlockSpec(right.shape, lambda s, g, tab: (0, 0)),
             ],
             out_specs=pl.BlockSpec((tile_rows, slots * BLK), lambda s, g, tab: (g, 0)),
-            scratch_shapes=[pltpu.VMEM((1, tile_rows, width), left.dtype)],
+            scratch_shapes=[
+                pltpu.VMEM((tile_rows, steps * CB * BLK), left.dtype),
+                pltpu.VMEM((1, tile_rows, right.shape[1]), left.dtype),
+            ],
         ),
     )(table, left, right)
 
@@ -166,9 +175,9 @@
         band_rows = lax.dynamic_slice_in_dim(neighbours, number * CB, CB, 0)
         band_cols = lax.dynamic_slice_in_dim(band_rows, col_index * slot_count, slot_count, 1) - col_index * CB
         right_tables.append(band_cols.reshape(-1))
-    left_dense = place(left_all, jnp.concatenate(left_tables), slot_count, CB, 1536, False)
     right_dense = place(band_all, jnp.concatenate(right_tables), slot_count, CB, 768, True)
-    return product_pick(left_dense, right_dense, own_cols.reshape(-1), 256)
+    table = jnp.concatenate(left_tables + [own_cols.reshape(-1)])
+    return fused_product(left_all, right_dense, table, slot_count, 256)
 
 
 def solution(mesh):

time: 227 us -> 223 us (0.982)
  Pallas kernels: 44.1 us -> 40.2 us
    pallas_call x2 -> x1, Pallas kernels: 24 us -> 6.35 us  [place(): pl.pallas_call(functools.partial(_place_kernel, src_blocks, dst_blocks, t...]
    pallas_call x1, Pallas kernels: 20.1 us -> 33.8 us  [fused_product(): pl.pallas_call(functools.partial(_fused_kernel, tile_rows, rows // BLK, s...]
where the time goes in v10:
time: 223 us; the launch traced here: 220 us
  waiting for transfers between devices  138 us (62%)
  Pallas kernels  40.2 us (18%)
  between operations  20.3 us (9%)
  other arithmetic  10.9 us (5%)
  starting transfers between devices  8.35 us (4%)
  local copies, waits for them, and re-layouts  2.39 us (1%)
    ppermute x5, waiting for transfers between devices, ring_shift(): return lax.ppermute(x, axis, [(i, (i + step) % size) for i in range(size)])  64.8 us
    all_gather x1, waiting for transfers between devices, on_device(): lax.all_gather(part, COL_AXES, axis=0, tiled=True)  50.2 us
    pallas_call x1, Pallas kernels, fused_product(): pl.pallas_call(functools.partial(_fused_kernel, tile_rows, rows // BLK, s...  33.8 us
    reduce_scatter x1, waiting for transfers between devices, on_device(): part = lax.psum_scatter(stacked, COL_AXES, scatter_dimension=0, tiled=True)  22.7 us
    ppermute x5, starting transfers between devices, ring_shift(): return lax.ppermute(x, axis, [(i, (i + step) % size) for i in range(size)])  8.3 us
    pallas_call x1, Pallas kernels, place(): pl.pallas_call(functools.partial(_place_kernel, src_blocks, dst_blocks, t...  6.35 us
    select_n x1, other arithmetic, on_device(): stacked = jnp.where(roots, density[None], jnp.zeros((), density.dtype))  4.71 us
  transfers between devices with their start and end apart: 7, of which 6 were waited for; matrix products, arithmetic and copies ran while one was open for 3% of the time, Pallas kernels for 3%

profile of v10, /device:TPU:32, one launch (start us, length us, event | category | flops | bytes accessed | tf_op | source)
XLA Modules:
  0.0 219.9 jit_solution(3235681238553261674)
XLA Ops:
  6.5 0.7 broadcast_compare_fusion
  7.3 4.7 %bitcast_select_fusion = bf16[6144,384]{1,0:T(8,128)(2,1)} fusion(pred[6144]{0:T(1024)(128)(4,1)S(1)} %broadcast_in_dim.54, bf16[3072,384]{1,0:T(8,128)(2,1)} %param.3), kind=kLoop, calls=%fused_computation | loop fusion | flops 2359296 | bytes 7084032 | tf_op jit(solution)/shard_map/jit(_where)/select_n | solution.py:151
  12.1 0.6 copy-done.1
  12.7 0.6 fusion.5
  17.8 0.2 select_bitcast_fusion.1
  18.1 0.1 pad_maximum_fusion
  18.2 1.9 collective-permute-start
  20.1 25.9 %collective-permute-done = bf16[2,768,384]{2,1,0:T(8,128)(2,1)S(1)} collective-permute-done((bf16[2,768,384]{2,1,0:T(8,128)(2,1)S(1)}, bf16[2,768,384]{2,1,0:T(8,128)(2,1)S(1)}, u32[]{:S(2)}, u32[]{:S(2)}) %collective-permute-start) | collective-permute-done | bytes 1179680 | tf_op jit(solution)/shard_map/ppermute | solution.py:118
  46.0 0.2 broadcast_select_fusion
  46.2 3.1 %collective-permute-start.2 = (bf16[2,768,384]{2,1,0:T(8,128)(2,1)S(1)}, bf16[2,768,384]{2,1,0:T(8,128)(2,1)S(1)}, u32[]{:S(2)}, u32[]{:S(2)}) collective-permute-start(bf16[2,768,384]{2,1,0:T(8,128)(2,1)S(1)} %broadcast_select_fusion), channel_id=1, source_target_pairs={{0,96},{32,0},{64,32},{96,64},{1,97},{33,1},{65,33},{97,65},{2,98}... | collective-permute-start | bytes 3538952 | tf_op jit(solution)/shard_map/ppermute | solution.py:118
  49.3 24.4 %collective-permute-done.2 = bf16[2,768,384]{2,1,0:T(8,128)(2,1)S(1)} collective-permute-done((bf16[2,768,384]{2,1,0:T(8,128)(2,1)S(1)}, bf16[2,768,384]{2,1,0:T(8,128)(2,1)S(1)}, u32[]{:S(2)}, u32[]{:S(2)}) %collective-permute-start.2) | collective-permute-done | bytes 1179680 | tf_op jit(solution)/shard_map/ppermute | solution.py:118
  73.7 3.4 %collective-permute-done.1 = bf16[2,768,384]{2,1,0:T(8,128)(2,1)S(1)} collective-permute-done((bf16[2,768,384]{2,1,0:T(8,128)(2,1)S(1)}, bf16[2,768,384]{2,1,0:T(8,128)(2,1)S(1)}, u32[]{:S(2)}, u32[]{:S(2)}) %collective-permute-start.1) | collective-permute-done | bytes 1179680 | tf_op jit(solution)/shard_map/ppermute | solution.py:118
  77.1 0.3 select_select_fusion
  77.4 0.1 fusion.4
  77.7 3.2 %collective-permute-start.4 = (bf16[2,384,384]{2,1,0:T(8,128)(2,1)S(1)}, bf16[2,384,384]{2,1,0:T(8,128)(2,1)S(1)}, u32[]{:S(2)}, u32[]{:S(2)}) collective-permute-start(bf16[2,384,384]{2,1,0:T(8,128)(2,1)S(1)} %get-tuple-element.15), channel_id=1, source_target_pairs={{0,96},{32,0},{64,32},{96,64},{1,97},{33,1},{65,33},{97,65},{2,98}... | collective-permute-start | bytes 1769480 | tf_op jit(solution)/shard_map/ppermute | solution.py:118
  80.9 11.2 %collective-permute-done.3 = bf16[2,384,384]{2,1,0:T(8,128)(2,1)S(1)} collective-permute-done((bf16[2,384,384]{2,1,0:T(8,128)(2,1)S(1)}, bf16[2,384,384]{2,1,0:T(8,128)(2,1)S(1)}, u32[]{:S(2)}, u32[]{:S(2)}) %collective-permute-start.3) | collective-permute-done | bytes 589856 | tf_op jit(solution)/shard_map/ppermute | solution.py:118
  92.0 1.5 maximum_select_fusion.values
  93.6 22.7 %reduce-scatter.2.cloned.1.call-done = bf16[192,384]{1,0:T(8,128)(2,1)} async-done(((bf16[6144,384]{1,0:T(8,128)(2,1)}), bf16[192,384]{1,0:T(8,128)(2,1)}) %reduce-scatter.2.cloned.1.call-update) | async-done | bytes 147472 | tf_op jit(solution)/shard_map/reduce_scatter | solution.py:160
  118.6 0.9 dynamic-slice_subtract_fusion.1
  119.4 0.1 copy.9
  119.6 0.1 copy.10
  119.8 0.9 dynamic-slice_subtract_fusion.4
  120.8 0.1 reshape.30
  120.9 0.1 copy.8
  121.0 0.1 reshape.32
  121.1 0.1 copy.7
  121.2 0.1 reshape.31
  121.4 0.7 pad_add_fusion.1.table
  122.0 0.7 pad_add_fusion.table
  122.7 6.4 %shard_map.37.right = bf16[1536,768]{1,0:T(8,128)(2,1)} custom-call(s32[144]{0:T(256)} %pad_add_fusion.1.table, bf16[2,768,384]{2,1,0:T(8,128)(2,1)} %maximum_select_fusion.values), custom_call_target="tpu_custom_call" | custom-call | tf_op jit(solution)/shard_map/pallas_call | solution.py:105
  129.0 50.2 %all-gather.2.cloned.1.call-done = bf16[6144,384]{1,0:T(8,128)(2,1)} async-done(((bf16[192,384]{1,0:T(8,128)(2,1)}), bf16[6144,384]{1,0:T(8,128)(2,1)}) %all-gather.2.cloned.1.call-update) | async-done | bytes 4718608 | tf_op jit(solution)/shard_map/all_gather | solution.py:167
  179.3 33.8 %shard_map.38 = bf16[3072,384]{1,0:T(8,128)(2,1)} custom-call(s32[864]{0:T(1024)} %pad_add_fusion.table, bf16[2,3072,384]{2,1,0:T(8,128)(2,1)} %bitcast.9, bf16[1536,768]{1,0:T(8,128)(2,1)} %shard_map.37.right), custom_call_target="tpu_custom_call" | custom-call | tf_op jit(solution)/shard_map/pallas_call | solution.py:77
  (17 shorter events, 0.6 us)
Async XLA Ops:
  6.5 109.7 %reduce-scatter.2.cloned.1.call-start = ((), (), s32[]{:S(2)}) async-start(), calls=%async_computation.1 | async-start | bytes 4866048 | tf_op jit(solution)/shard_map/reduce_scatter | solution.py:160
  12.0 0.7 copy-start.1
  12.0 5.8 %copy-start = (bf16[3072,384]{1,0:T(8,128)(2,1)S(1)}, bf16[3072,384]{1,0:T(8,128)(2,1)}, u32[]{:S(2)}) copy-start(bf16[3072,384]{1,0:T(8,128)(2,1)} %param.3) | copy-start | bytes 7077892
  12.1 167.2 %all-gather.2.cloned.1.call-start = ((), (), s32[]{:S(2)}) async-start(), calls=%async_computation.2 | async-start | bytes 4866048 | tf_op jit(solution)/shard_map/all_gather | solution.py:167
  18.2 27.8 %collective-permute-start = (bf16[2,768,384]{2,1,0:T(8,128)(2,1)S(1)}, bf16[2,768,384]{2,1,0:T(8,128)(2,1)S(1)}, u32[]{:S(2)}, u32[]{:S(2)}) collective-permute-start(bf16[2,768,384]{2,1,0:T(8,128)(2,1)S(1)} %pad_maximum_fusion), channel_id=1, source_target_pairs={{0,128},{128,0},{1,129},{129,1},{2,130},{130,2},{3,131},{131,3},{4... | collective-permute-start | bytes 3538952 | tf_op jit(solution)/shard_map/ppermute | solution.py:118
  46.2 27.5 %collective-permute-start.2 = (bf16[2,768,384]{2,1,0:T(8,128)(2,1)S(1)}, bf16[2,768,384]{2,1,0:T(8,128)(2,1)S(1)}, u32[]{:S(2)}, u32[]{:S(2)}) collective-permute-start(bf16[2,768,384]{2,1,0:T(8,128)(2,1)S(1)} %broadcast_select_fusion), channel_id=1, source_target_pairs={{0,96},{32,0},{64,32},{96,64},{1,97},{33,1},{65,33},{97,65},{2,98}... | collective-permute-start | bytes 3538952 | tf_op jit(solution)/shard_map/ppermute | solution.py:118
  49.3 27.8 %collective-permute-start.1 = (bf16[2,768,384]{2,1,0:T(8,128)(2,1)S(1)}, bf16[2,768,384]{2,1,0:T(8,128)(2,1)S(1)}, u32[]{:S(2)}, u32[]{:S(2)}) collective-permute-start(bf16[2,768,384]{2,1,0:T(8,128)(2,1)S(1)} %broadcast_select_fusion), channel_id=1, source_target_pairs={{0,32},{32,64},{64,96},{96,0},{1,33},{33,65},{65,97},{97,1},{2,34}... | collective-permute-start | bytes 3538952 | tf_op jit(solution)/shard_map/ppermute | solution.py:118
  77.6 14.5 %collective-permute-start.3 = (bf16[2,384,384]{2,1,0:T(8,128)(2,1)S(1)}, bf16[2,384,384]{2,1,0:T(8,128)(2,1)S(1)}, u32[]{:S(2)}, u32[]{:S(2)}) collective-permute-start(bf16[2,384,384]{2,1,0:T(8,128)(2,1)S(1)} %get-tuple-element.14), channel_id=1, source_target_pairs={{0,32},{32,64},{64,96},{96,0},{1,33},{33,65},{65,97},{97,1},{2,34}... | collective-permute-start | bytes 1769480 | tf_op jit(solution)/shard_map/ppermute | solution.py:118
  77.7 14.4 %collective-permute-start.4 = (bf16[2,384,384]{2,1,0:T(8,128)(2,1)S(1)}, bf16[2,384,384]{2,1,0:T(8,128)(2,1)S(1)}, u32[]{:S(2)}, u32[]{:S(2)}) collective-permute-start(bf16[2,384,384]{2,1,0:T(8,128)(2,1)S(1)} %get-tuple-element.15), channel_id=1, source_target_pairs={{0,96},{32,0},{64,32},{96,64},{1,97},{33,1},{65,33},{97,65},{2,98}... | collective-permute-start | bytes 1769480 | tf_op jit(solution)/shard_map/ppermute | solution.py:118
Sparse Core Ops, SparseCore 0:
  12.2 104.0 reduce-scatter.1
  118.8 60.4 all-gather.1

commit v11 on v10

--- a/solution.py
+++ b/solution.py
@@ -177,7 +177,7 @@
         right_tables.append(band_cols.reshape(-1))
     right_dense = place(band_all, jnp.concatenate(right_tables), slot_count, CB, 768, True)
     table = jnp.concatenate(left_tables + [own_cols.reshape(-1)])
-    return fused_product(left_all, right_dense, table, slot_count, 256)
+    return fused_product(left_all, right_dense, table, slot_count, 512)
 
 
 def solution(mesh):

time: 223 us -> 222 us (level)
  no operation moved by 1% of the time
where the time goes in v11:
time: 222 us; the launch traced here: 219 us
  waiting for transfers between devices  138 us (62%)
  Pallas kernels  39.2 us (18%)
  between operations  20.3 us (9%)
  other arithmetic  10.9 us (5%)
  starting transfers between devices  8.35 us (4%)
  local copies, waits for them, and re-layouts  2.39 us (1%)
    ppermute x5, waiting for transfers between devices, ring_shift(): return lax.ppermute(x, axis, [(i, (i + step) % size) for i in range(size)])  64.8 us
    all_gather x1, waiting for transfers between devices, on_device(): lax.all_gather(part, COL_AXES, axis=0, tiled=True)  50.2 us
    pallas_call x1, Pallas kernels, fused_product(): pl.pallas_call(functools.partial(_fused_kernel, tile_rows, rows // BLK, s...  32.8 us
    reduce_scatter x1, waiting for transfers between devices, on_device(): part = lax.psum_scatter(stacked, COL_AXES, scatter_dimension=0, tiled=True)  22.7 us
    ppermute x5, starting transfers between devices, ring_shift(): return lax.ppermute(x, axis, [(i, (i + step) % size) for i in range(size)])  8.3 us
    pallas_call x1, Pallas kernels, place(): pl.pallas_call(functools.partial(_place_kernel, src_blocks, dst_blocks, t...  6.35 us
    select_n x1, other arithmetic, on_device(): stacked = jnp.where(roots, density[None], jnp.zeros((), density.dtype))  4.71 us
  transfers between devices with their start and end apart: 7, of which 6 were waited for; matrix products, arithmetic and copies ran while one was open for 3% of the time, Pallas kernels for 3%

profile of v11, /device:TPU:32, one launch (start us, length us, event | category | flops | bytes accessed | tf_op | source)
XLA Modules:
  0.0 218.9 jit_solution(7886235585509010388)
XLA Ops:
  6.5 0.7 broadcast_compare_fusion
  7.3 4.7 %bitcast_select_fusion = bf16[6144,384]{1,0:T(8,128)(2,1)} fusion(pred[6144]{0:T(1024)(128)(4,1)S(1)} %broadcast_in_dim.54, bf16[3072,384]{1,0:T(8,128)(2,1)} %param.3), kind=kLoop, calls=%fused_computation | loop fusion | flops 2359296 | bytes 7084032 | tf_op jit(solution)/shard_map/jit(_where)/select_n | solution.py:151
  12.1 0.6 copy-done.1
  12.7 0.6 fusion.5
  17.8 0.2 select_bitcast_fusion.1
  18.1 0.1 pad_maximum_fusion
  18.2 1.9 collective-permute-start
  20.1 25.9 %collective-permute-done = bf16[2,768,384]{2,1,0:T(8,128)(2,1)S(1)} collective-permute-done((bf16[2,768,384]{2,1,0:T(8,128)(2,1)S(1)}, bf16[2,768,384]{2,1,0:T(8,128)(2,1)S(1)}, u32[]{:S(2)}, u32[]{:S(2)}) %collective-permute-start) | collective-permute-done | bytes 1179680 | tf_op jit(solution)/shard_map/ppermute | solution.py:118
  46.0 0.2 broadcast_select_fusion
  46.2 3.1 %collective-permute-start.2 = (bf16[2,768,384]{2,1,0:T(8,128)(2,1)S(1)}, bf16[2,768,384]{2,1,0:T(8,128)(2,1)S(1)}, u32[]{:S(2)}, u32[]{:S(2)}) collective-permute-start(bf16[2,768,384]{2,1,0:T(8,128)(2,1)S(1)} %broadcast_select_fusion), channel_id=1, source_target_pairs={{0,96},{32,0},{64,32},{96,64},{1,97},{33,1},{65,33},{97,65},{2,98}... | collective-permute-start | bytes 3538952 | tf_op jit(solution)/shard_map/ppermute | solution.py:118
  49.3 24.4 %collective-permute-done.2 = bf16[2,768,384]{2,1,0:T(8,128)(2,1)S(1)} collective-permute-done((bf16[2,768,384]{2,1,0:T(8,128)(2,1)S(1)}, bf16[2,768,384]{2,1,0:T(8,128)(2,1)S(1)}, u32[]{:S(2)}, u32[]{:S(2)}) %collective-permute-start.2) | collective-permute-done | bytes 1179680 | tf_op jit(solution)/shard_map/ppermute | solution.py:118
  73.7 3.4 %collective-permute-done.1 = bf16[2,768,384]{2,1,0:T(8,128)(2,1)S(1)} collective-permute-done((bf16[2,768,384]{2,1,0:T(8,128)(2,1)S(1)}, bf16[2,768,384]{2,1,0:T(8,128)(2,1)S(1)}, u32[]{:S(2)}, u32[]{:S(2)}) %collective-permute-start.1) | collective-permute-done | bytes 1179680 | tf_op jit(solution)/shard_map/ppermute | solution.py:118
  77.1 0.3 select_select_fusion
  77.4 0.1 fusion.4
  77.7 3.2 %collective-permute-start.4 = (bf16[2,384,384]{2,1,0:T(8,128)(2,1)S(1)}, bf16[2,384,384]{2,1,0:T(8,128)(2,1)S(1)}, u32[]{:S(2)}, u32[]{:S(2)}) collective-permute-start(bf16[2,384,384]{2,1,0:T(8,128)(2,1)S(1)} %get-tuple-element.15), channel_id=1, source_target_pairs={{0,96},{32,0},{64,32},{96,64},{1,97},{33,1},{65,33},{97,65},{2,98}... | collective-permute-start | bytes 1769480 | tf_op jit(solution)/shard_map/ppermute | solution.py:118
  80.9 11.2 %collective-permute-done.3 = bf16[2,384,384]{2,1,0:T(8,128)(2,1)S(1)} collective-permute-done((bf16[2,384,384]{2,1,0:T(8,128)(2,1)S(1)}, bf16[2,384,384]{2,1,0:T(8,128)(2,1)S(1)}, u32[]{:S(2)}, u32[]{:S(2)}) %collective-permute-start.3) | collective-permute-done | bytes 589856 | tf_op jit(solution)/shard_map/ppermute | solution.py:118
  92.0 1.5 maximum_select_fusion.values
  93.6 22.7 %reduce-scatter.2.cloned.1.call-done = bf16[192,384]{1,0:T(8,128)(2,1)} async-done(((bf16[6144,384]{1,0:T(8,128)(2,1)}), bf16[192,384]{1,0:T(8,128)(2,1)}) %reduce-scatter.2.cloned.1.call-update) | async-done | bytes 147472 | tf_op jit(solution)/shard_map/reduce_scatter | solution.py:160
  118.6 0.9 dynamic-slice_subtract_fusion.1
  119.4 0.1 copy.9
  119.6 0.1 copy.10
  119.8 0.9 dynamic-slice_subtract_fusion.4
  120.8 0.1 reshape.30
  120.9 0.1 copy.8
  121.0 0.1 reshape.32
  121.1 0.1 copy.7
  121.2 0.1 reshape.31
  121.3 0.7 pad_add_fusion.1.table
  122.0 0.7 pad_add_fusion.table
  122.6 6.4 %shard_map.37.right = bf16[1536,768]{1,0:T(8,128)(2,1)} custom-call(s32[144]{0:T(256)} %pad_add_fusion.1.table, bf16[2,768,384]{2,1,0:T(8,128)(2,1)} %maximum_select_fusion.values), custom_call_target="tpu_custom_call" | custom-call | tf_op jit(solution)/shard_map/pallas_call | solution.py:105
  129.0 50.2 %all-gather.2.cloned.1.call-done = bf16[6144,384]{1,0:T(8,128)(2,1)} async-done(((bf16[192,384]{1,0:T(8,128)(2,1)}), bf16[6144,384]{1,0:T(8,128)(2,1)}) %all-gather.2.cloned.1.call-update) | async-done | bytes 4718608 | tf_op jit(solution)/shard_map/all_gather | solution.py:167
  179.2 32.8 %shard_map.38 = bf16[3072,384]{1,0:T(8,128)(2,1)} custom-call(s32[864]{0:T(1024)} %pad_add_fusion.table, bf16[2,3072,384]{2,1,0:T(8,128)(2,1)} %bitcast.9, bf16[1536,768]{1,0:T(8,128)(2,1)} %shard_map.37.right), custom_call_target="tpu_custom_call" | custom-call | tf_op jit(solution)/shard_map/pallas_call | solution.py:77
  (17 shorter events, 0.6 us)
Async XLA Ops:
  6.5 109.7 %reduce-scatter.2.cloned.1.call-start = ((), (), s32[]{:S(2)}) async-start(), calls=%async_computation.1 | async-start | bytes 4866048 | tf_op jit(solution)/shard_map/reduce_scatter | solution.py:160
  12.0 0.7 copy-start.1
  12.0 5.8 %copy-start = (bf16[3072,384]{1,0:T(8,128)(2,1)S(1)}, bf16[3072,384]{1,0:T(8,128)(2,1)}, u32[]{:S(2)}) copy-start(bf16[3072,384]{1,0:T(8,128)(2,1)} %param.3) | copy-start | bytes 7077892
  12.1 167.1 %all-gather.2.cloned.1.call-start = ((), (), s32[]{:S(2)}) async-start(), calls=%async_computation.2 | async-start | bytes 4866048 | tf_op jit(solution)/shard_map/all_gather | solution.py:167
  18.2 27.8 %collective-permute-start = (bf16[2,768,384]{2,1,0:T(8,128)(2,1)S(1)}, bf16[2,768,384]{2,1,0:T(8,128)(2,1)S(1)}, u32[]{:S(2)}, u32[]{:S(2)}) collective-permute-start(bf16[2,768,384]{2,1,0:T(8,128)(2,1)S(1)} %pad_maximum_fusion), channel_id=1, source_target_pairs={{0,128},{128,0},{1,129},{129,1},{2,130},{130,2},{3,131},{131,3},{4... | collective-permute-start | bytes 3538952 | tf_op jit(solution)/shard_map/ppermute | solution.py:118
  46.2 27.5 %collective-permute-start.2 = (bf16[2,768,384]{2,1,0:T(8,128)(2,1)S(1)}, bf16[2,768,384]{2,1,0:T(8,128)(2,1)S(1)}, u32[]{:S(2)}, u32[]{:S(2)}) collective-permute-start(bf16[2,768,384]{2,1,0:T(8,128)(2,1)S(1)} %broadcast_select_fusion), channel_id=1, source_target_pairs={{0,96},{32,0},{64,32},{96,64},{1,97},{33,1},{65,33},{97,65},{2,98}... | collective-permute-start | bytes 3538952 | tf_op jit(solution)/shard_map/ppermute | solution.py:118
  49.3 27.8 %collective-permute-start.1 = (bf16[2,768,384]{2,1,0:T(8,128)(2,1)S(1)}, bf16[2,768,384]{2,1,0:T(8,128)(2,1)S(1)}, u32[]{:S(2)}, u32[]{:S(2)}) collective-permute-start(bf16[2,768,384]{2,1,0:T(8,128)(2,1)S(1)} %broadcast_select_fusion), channel_id=1, source_target_pairs={{0,32},{32,64},{64,96},{96,0},{1,33},{33,65},{65,97},{97,1},{2,34}... | collective-permute-start | bytes 3538952 | tf_op jit(solution)/shard_map/ppermute | solution.py:118
  77.6 14.5 %collective-permute-start.3 = (bf16[2,384,384]{2,1,0:T(8,128)(2,1)S(1)}, bf16[2,384,384]{2,1,0:T(8,128)(2,1)S(1)}, u32[]{:S(2)}, u32[]{:S(2)}) collective-permute-start(bf16[2,384,384]{2,1,0:T(8,128)(2,1)S(1)} %get-tuple-element.14), channel_id=1, source_target_pairs={{0,32},{32,64},{64,96},{96,0},{1,33},{33,65},{65,97},{97,1},{2,34}... | collective-permute-start | bytes 1769480 | tf_op jit(solution)/shard_map/ppermute | solution.py:118
  77.7 14.4 %collective-permute-start.4 = (bf16[2,384,384]{2,1,0:T(8,128)(2,1)S(1)}, bf16[2,384,384]{2,1,0:T(8,128)(2,1)S(1)}, u32[]{:S(2)}, u32[]{:S(2)}) collective-permute-start(bf16[2,384,384]{2,1,0:T(8,128)(2,1)S(1)} %get-tuple-element.15), channel_id=1, source_target_pairs={{0,96},{32,0},{64,32},{96,64},{1,97},{33,1},{65,33},{97,65},{2,98}... | collective-permute-start | bytes 1769480 | tf_op jit(solution)/shard_map/ppermute | solution.py:118
Sparse Core Ops, SparseCore 0:
  12.2 104.0 reduce-scatter.1
  118.8 60.3 all-gather.1
